TPU v7x, 768 devices: a whole 4x8x12 slice. The times are simulated.
768 devices in a mesh: dp: 192 (over y, z, core), mp: 4 (over x).
Axes of the slice: x: 4, y: 8, z: 12, core: 2. Of those that a mesh axis runs over, the one named last changes fastest.
Arguments:
- tokens: bfloat16 [24576, 4096], P('dp'), may hold values from -6 to 6
- blocks: bfloat16 [96, 128, 128], P('mp'), may hold values from -0.5 to 0.5
- block_row: int32 [96], P('mp'), may hold values from -1 to 31, as said below
- block_col: int32 [96], P('mp'), may hold values from -1 to 127, as said below
- cotangent: bfloat16 [24576, 16384], P('dp', 'mp'), may hold values from -6 to 6
Outputs:
- activation: bfloat16 [24576, 16384], P('dp', 'mp')
- input_grad: bfloat16 [24576, 4096], P('dp', 'mp')
- weight_grad: float32 [16, 768, 128], P('mp', 'dp')
Inputs may be any that keep to these rules, and one draw needn't show every extreme that they name: `block_row`: slots form 4 x 4 groups of 6: slot (m * 4 + q) * 6 + k. In each group the live slots come first and the others hold -1 in both lists. A live slot of group (m, q) has its column block in q * 32 to q * 32 + 31, and all live slots of one row block lie in groups of one m. No pair of row and column block repeats. For some q all 4 groups (m, q) are full. `block_col`: as for block_row: the two lists are drawn together.
All inputs are finite; a program needn't handle non-finite values.
Results may differ from a plain program's by a relative error of at most 0.0075.
Values may be sent and summed in bfloat16 or wider, within the bound.
No kernel may reach another device: no remote copies, remote signals or barrier semaphores. Data moves between devices by JAX's collectives and lax.ppermute only.
A program may use at most 32 MiB of HBM per device.

v0:
```python
import jax
import jax.numpy as jnp
from jax import lax
from jax.sharding import PartitionSpec as P


def gelu_tanh(inputs):
    return jax.nn.gelu(inputs, approximate=True)


def body(tokens, blocks, block_row, block_col, cotangent):
    mp_count = lax.axis_size("mp")
    token_count = tokens.shape[0]
    block_size = blocks.shape[1]
    row_blocks = tokens.shape[1] // block_size
    slot_cap = blocks.shape[0] // mp_count
    col_blocks = cotangent.shape[1] // block_size
    column_here = lax.axis_index("mp")
    spread = tokens.reshape(token_count, row_blocks, block_size)
    w_groups = blocks.reshape(mp_count, slot_cap, block_size, block_size)
    row_groups = jnp.maximum(block_row, 0).reshape(mp_count, slot_cap)
    col_groups = block_col.reshape(mp_count, slot_cap)
    picked_x = jnp.take(spread, row_groups, axis=1)
    live_mask = (col_groups >= 0).astype(jnp.float32)
    own_parts = jnp.einsum(
        "tmck,mckn->mctn", picked_x, w_groups, preferred_element_type=jnp.float32
    )
    own_parts = (own_parts * live_mask[:, :, None, None]).astype(jnp.bfloat16)
    partials, got_cols = (
        lax.all_to_all(own_parts, "mp", split_axis=0, concat_axis=0, tiled=True),
        lax.all_to_all(col_groups, "mp", split_axis=0, concat_axis=0, tiled=True),
    )
    local_col = got_cols - column_here * col_blocks
    onehot = (local_col[:, :, None] == jnp.arange(col_blocks)[None, None, :]).astype(jnp.bfloat16)
    pre_act = jnp.einsum("mctn,mcj->tjn", partials, onehot, preferred_element_type=jnp.float32)
    pre_act = pre_act.reshape(token_count, col_blocks * block_size)
    activation_f, pullback = jax.vjp(gelu_tanh, pre_act)
    activation = activation_f.astype(jnp.bfloat16)
    pre_grad = pullback(cotangent.astype(jnp.float32))[0].astype(jnp.bfloat16)
    pre_grad = pre_grad.reshape(token_count, col_blocks, block_size)
    returned = jnp.einsum(
        "tjn,mcj->mctn", pre_grad, onehot, preferred_element_type=jnp.float32
    ).astype(jnp.bfloat16)
    returned = lax.all_to_all(returned, "mp", split_axis=0, concat_axis=0, tiled=True)
    slot_live = col_groups >= 0
    input_terms = jnp.einsum(
        "mctn,mckn->mctk", returned, w_groups, preferred_element_type=jnp.float32
    )
    row_onehot = (
        (row_groups[:, :, None] == jnp.arange(row_blocks)[None, None, :]) & slot_live[:, :, None]
    ).astype(jnp.float32)
    input_partial = jnp.einsum(
        "mctk,mcr->trk", input_terms, row_onehot, precision=lax.Precision.HIGHEST
    )
    input_partial = input_partial.reshape(token_count, row_blocks * block_size)
    input_grad = lax.psum_scatter(
        input_partial.astype(jnp.bfloat16), "mp", scatter_dimension=1, tiled=True
    )
    weight_terms = jnp.einsum(
        "tmck,mctn->mckn", picked_x, returned, preferred_element_type=jnp.float32
    )
    weight_terms = weight_terms.reshape(mp_count, slot_cap * block_size, block_size)
    summed = lax.psum_scatter(weight_terms, "dp", scatter_dimension=1, tiled=True)
    return (activation, input_grad, summed)


def solution(mesh):
    placed = (P("dp", None), P("mp", None, None), P("mp"), P("mp"), P("dp", "mp"))
    return jax.shard_map(
        body,
        mesh=mesh,
        in_specs=placed,
        out_specs=(P("dp", "mp"), P("dp", "mp"), P("mp", "dp", None)),
        check_vma=False,
    )
```

profile of v0, /device:TPU:1, one launch (start us, length us, event | category | flops | bytes accessed | tf_op | source)
XLA Modules:
  0.0 380.5 jit_solution(7013256938361834925)
XLA Ops:
  8.0 0.0 copy-start
  8.0 1.4 all_to_all.12
  9.4 4.8 %all-to-all-start = ((s32[4,1,6]{2,1,0:T(1,128)}), s32[4,1,6]{2,1,0:T(1,128)S(1)}, u32[]{:S(2)}, u32[]{:S(2)}) async-start(s32[4,1,6]{2,1,0:T(1,128)} %bitcast), calls=%async_computation | async-start | bytes 4096 | tf_op jit(solution)/shard_map/all_to_all | solution.py:31
  14.2 0.7 broadcast_maximum_fusion
  14.9 0.1 reshape.87
  15.0 0.1 reshape.89
  15.1 0.7 broadcast_compare_fusion
  15.7 0.1 reshape.96
  15.8 2.3 copy.21
  18.1 1.6 copy.22
  19.7 0.7 gather_fusion
  20.4 0.4 copy.23
  20.8 0.1 ge.24
  20.9 1.4 multiply_convert_fusion
  22.3 4.4 %all-to-all-start.1 = ((bf16[4,6,128,128]{3,2,1,0:T(8,128)(2,1)}), bf16[4,6,128,128]{3,2,1,0:T(8,128)(2,1)S(1)}, u32[]{:S(2)}, u32[]{:S(2)}) async-start(bf16[4,6,128,128]{3,2,1,0:T(8,128)(2,1)} %multiply_convert_fusion), calls=%async_computation.1 | async-start | bytes 1572864 | tf_op jit(solution)/shard_map/all_to_all | solution.py:30
  26.7 8.3 %all-to-all-done.1 = bf16[4,6,128,128]{3,2,1,0:T(8,128)(2,1)S(1)} async-done(((bf16[4,6,128,128]{3,2,1,0:T(8,128)(2,1)}), bf16[4,6,128,128]{3,2,1,0:T(8,128)(2,1)S(1)}, u32[]{:S(2)}, u32[]{:S(2)}) %all-to-all-start.1) | async-done | bytes 786464 | tf_op jit(solution)/shard_map/all_to_all | solution.py:30
  35.0 1.0 fusion.15
  36.1 3.3 fusion.17
  39.3 0.2 copy.35
  39.6 0.4 convolution_convert_fusion
  40.0 0.2 copy.26
  40.2 10.7 %all_to_all.19 = bf16[4,6,128,128]{3,2,1,0:T(8,128)(2,1)S(1)} all-to-all(bf16[4,6,128,128]{3,2,1,0:T(8,128)(2,1)S(1)} %copy.26), channel_id=1, replica_groups=mesh['dp'=192,'mp'=4] {'mp'}, dimensions={0} | all-to-all | bytes 1572864 | tf_op jit(solution)/shard_map/all_to_all | solution.py:44
  51.0 1.6 fusion.18
  52.5 0.0 all-reduce.3.cloned.1.call-update
  52.6 0.0 reduce-scatter.3.cloned.1.call-start
  52.6 0.7 fusion.36
  53.3 2.7 bitcast_convert_fusion
  56.0 1.4 copy.53
  57.5 0.0 reduce-scatter.3.cloned.1.call-update
  57.5 1.3 dynamic-slice
  59.4 312.3 %all-reduce.3.cloned.1.call-done = f32[4,768,128]{2,1,0:T(8,128)} async-done(((f32[4,768,128]{2,1,0:T(8,128)}), f32[4,768,128]{2,1,0:T(8,128)}) %all-reduce.3.cloned.1.call-update) | async-done | bytes 1572880
  371.7 1.3 constant_dynamic-slice_fusion
  (11 shorter events, 0.0 us)
Async XLA Ops:
  8.0 12.9 %copy-start = (bf16[24,128,128]{2,1,0:T(8,128)(2,1)S(1)}, bf16[24,128,128]{2,1,0:T(8,128)(2,1)}, u32[]{:S(2)}) copy-start(bf16[24,128,128]{2,1,0:T(8,128)(2,1)} %param.6) | copy-start | bytes 2359300
  9.4 12.9 %all-to-all-start = ((s32[4,1,6]{2,1,0:T(1,128)}), s32[4,1,6]{2,1,0:T(1,128)S(1)}, u32[]{:S(2)}, u32[]{:S(2)}) async-start(s32[4,1,6]{2,1,0:T(1,128)} %bitcast), calls=%async_computation | async-start | bytes 4096 | tf_op jit(solution)/shard_map/all_to_all | solution.py:31
  22.3 13.8 %copy-start.1 = (bf16[128,4096]{1,0:T(8,128)(2,1)S(1)}, bf16[128,4096]{1,0:T(8,128)(2,1)}, u32[]{:S(2)}) copy-start(bf16[128,4096]{1,0:T(8,128)(2,1)} %param.9) | copy-start | bytes 3145732
  22.3 12.7 %all-to-all-start.1 = ((bf16[4,6,128,128]{3,2,1,0:T(8,128)(2,1)}), bf16[4,6,128,128]{3,2,1,0:T(8,128)(2,1)S(1)}, u32[]{:S(2)}, u32[]{:S(2)}) async-start(bf16[4,6,128,128]{3,2,1,0:T(8,128)(2,1)} %multiply_convert_fusion), calls=%async_computation.1 | async-start | bytes 1572864 | tf_op jit(solution)/shard_map/all_to_all | solution.py:30
  26.7 345.0 %all-reduce.3.cloned.1.call-start = ((), (), s32[]{:S(2)}) async-start(), calls=%async_computation.5 | async-start | bytes 3145728
  52.6 320.5 %reduce-scatter.3.cloned.1.call-start = ((), (), s32[]{:S(2)}) async-start(), calls=%async_computation.4 | async-start | bytes 1310720 | tf_op jit(solution)/shard_map/reduce_scatter | solution.py:56
Sparse Core Ops, SparseCore 0:
  52.7 318.9 all-reduce.2
Sparse Core Ops, SparseCore 1:
  57.6 41.9 reduce-scatter.2
where the time goes:
time: 381 us; the launch traced here: 380 us
  waiting for transfers between devices  321 us (84%)
  between operations  16.2 us (4%)
  local copies, waits for them, and re-layouts  11.1 us (3%)
  blocking collectives  10.7 us (3%)
  starting transfers between devices  9.25 us (2%)
  matrix products  7.86 us (2%)
  other arithmetic  4.62 us (1%)
    unnamed x3, waiting for transfers between devices  312 us
    all_to_all x1, blocking collectives, body(): lax.all_to_all(returned, 'mp', split_axis=0, concat_axis=0, tiled=True)  10.7 us
    all_to_all x1, waiting for transfers between devices, body(): lax.all_to_all(own_parts, 'mp', split_axis=0, concat_axis=0, tiled=True)  8.33 us
  transfers between devices with their start and end apart: 4, of which 2 were waited for; matrix products, arithmetic and copies ran while one was open for 4% of the time, Pallas kernels for 0%

commit v1 on v0

--- a/solution.py
+++ b/solution.py
@@ -1,7 +1,7 @@
 import jax
 import jax.numpy as jnp
 from jax import lax
-from jax.sharding import PartitionSpec as P
+from jax.sharding import Mesh, PartitionSpec as P
 
 
 def gelu_tanh(inputs):
@@ -60,16 +60,28 @@
         "tmck,mctn->mckn", picked_x, returned, preferred_element_type=jnp.float32
     )
     weight_terms = weight_terms.reshape(mp_count, slot_cap * block_size, block_size)
-    summed = lax.psum_scatter(weight_terms, "dp", scatter_dimension=1, tiled=True)
+    ny, nz, nc = lax.axis_size("y"), lax.axis_size("z"), lax.axis_size("c")
+    rows = slot_cap * block_size // (ny * nz * nc)
+    staged = weight_terms.reshape(mp_count, ny, nz, nc, rows, block_size)
+    staged = jnp.transpose(staged, (3, 2, 1, 4, 0, 5)).reshape(-1, mp_count, block_size)
+    for axis in ("c", "z", "y"):
+        staged = lax.psum_scatter(staged, axis, scatter_dimension=0, tiled=True)
+    summed = jnp.transpose(staged, (1, 0, 2))
     return (activation, input_grad, summed)
 
 
 def solution(mesh):
-    placed = (P("dp", None), P("mp", None, None), P("mp"), P("mp"), P("dp", "mp"))
+    dp_count, mp_count = mesh.devices.shape
+    y_count = len({d.coords[1] for d in mesh.devices.flat})
+    chip_cores = len({d.core_on_chip for d in mesh.devices.flat})
+    grid = mesh.devices.reshape(y_count, dp_count // (y_count * chip_cores), chip_cores, mp_count)
+    split = Mesh(grid, ("y", "z", "c", "mp"))
+    dp = ("y", "z", "c")
+    placed = (P(dp, None), P("mp", None, None), P("mp"), P("mp"), P(dp, "mp"))
     return jax.shard_map(
         body,
-        mesh=mesh,
+        mesh=split,
         in_specs=placed,
-        out_specs=(P("dp", "mp"), P("dp", "mp"), P("mp", "dp", None)),
+        out_specs=(P(dp, "mp"), P(dp, "mp"), P("mp", dp, None)),
         check_vma=False,
     )

time: 381 us -> 239 us (0.63)
  the two profiles are of different devices: /device:TPU:1 before, /device:TPU:2 now
where the time goes in v1:
time: 239 us
  waiting for transfers between devices  169 us (71%)
  starting transfers between devices  17.8 us (7%)
  between operations  15.9 us (7%)
  local copies, waits for them, and re-layouts  12.7 us (5%)
  blocking collectives  11.9 us (5%)
  matrix products  6.68 us (3%)
  other arithmetic  4.62 us (2%)
    reduce_scatter x2, waiting for transfers between devices, body(): staged = lax.psum_scatter(staged, axis, scatter_dimension=0, tiled=True)  83.8 us
    unnamed x5, waiting for transfers between devices  77.1 us
    all_to_all x1, starting transfers between devices, body(): lax.all_to_all(col_groups, 'mp', split_axis=0, concat_axis=0, tiled=True)  12.7 us
    all_to_all x1, blocking collectives, body(): lax.all_to_all(returned, 'mp', split_axis=0, concat_axis=0, tiled=True)  11.9 us
    all_to_all x1, waiting for transfers between devices, body(): lax.all_to_all(own_parts, 'mp', split_axis=0, concat_axis=0, tiled=True)  8.02 us
    unnamed x8, local copies, waits for them, and re-layouts  5.2 us
    all_to_all x1, starting transfers between devices, body(): lax.all_to_all(own_parts, 'mp', split_axis=0, concat_axis=0, tiled=True)  4.93 us
  transfers between devices with their start and end apart: 6, of which 4 were waited for; matrix products, arithmetic and copies ran while one was open for 6% of the time, Pallas kernels for 0%

profile of v1, /device:TPU:2, one launch (start us, length us, event | category | flops | bytes accessed | tf_op | source)
XLA Modules:
  0.0 238.5 jit_solution(11011365326216828013)
XLA Ops:
  8.0 1.4 all_to_all.12
  9.4 12.7 %all-to-all-start = ((s32[4,1,6]{2,1,0:T(1,128)}), s32[4,1,6]{2,1,0:T(1,128)S(1)}, u32[]{:S(2)}, u32[]{:S(2)}) async-start(s32[4,1,6]{2,1,0:T(1,128)} %bitcast), calls=%async_computation | async-start | bytes 4096 | tf_op jit(solution)/shard_map/all_to_all | solution.py:31
  22.1 0.7 broadcast_maximum_fusion
  22.8 0.1 reshape.87
  22.8 0.1 reshape.89
  22.9 0.7 broadcast_compare_fusion
  23.6 0.1 reshape.96
  23.7 2.3 copy.24
  26.0 1.6 copy.25
  27.6 0.7 gather_fusion
  28.3 0.4 copy.26
  28.7 0.1 ge.24
  28.8 1.4 multiply_convert_fusion
  30.2 4.9 %all-to-all-start.1 = ((bf16[4,6,128,128]{3,2,1,0:T(8,128)(2,1)}), bf16[4,6,128,128]{3,2,1,0:T(8,128)(2,1)S(1)}, u32[]{:S(2)}, u32[]{:S(2)}) async-start(bf16[4,6,128,128]{3,2,1,0:T(8,128)(2,1)} %multiply_convert_fusion), calls=%async_computation.1 | async-start | bytes 1572864 | tf_op jit(solution)/shard_map/all_to_all | solution.py:30
  35.1 8.0 %all-to-all-done.1 = bf16[4,6,128,128]{3,2,1,0:T(8,128)(2,1)S(1)} async-done(((bf16[4,6,128,128]{3,2,1,0:T(8,128)(2,1)}), bf16[4,6,128,128]{3,2,1,0:T(8,128)(2,1)S(1)}, u32[]{:S(2)}, u32[]{:S(2)}) %all-to-all-start.1) | async-done | bytes 786464 | tf_op jit(solution)/shard_map/all_to_all | solution.py:30
  43.1 1.0 fusion.15
  44.2 3.3 %fusion.17 = (bf16[16,8,32,128]{3,1,2,0:T(8,128)(2,1)S(1)}, bf16[128,4096]{1,0:T(8,128)(2,1)}) fusion(f32[16,8,32,128]{3,2,1,0:T(8,128)S(1)} %bitcast.69, bf16[128,4096]{1,0:T(8,128)(2,1)S(1)} %copy-done.1), kind=kLoop, calls=%fused_computation.25 | loop fusion | flops 12058624 | bytes 5242880
  47.5 0.2 copy.39
  47.7 0.4 convolution_convert_fusion
  48.2 0.2 copy.29
  48.3 11.9 %all_to_all.19 = bf16[4,6,128,128]{3,2,1,0:T(8,128)(2,1)S(1)} all-to-all(bf16[4,6,128,128]{3,2,1,0:T(8,128)(2,1)S(1)} %copy.29), channel_id=1, replica_groups=mesh['y'=8,'z'=12,'c'=2,'mp'=4] {'mp'}, dimensions={0} | all-to-all | bytes 1572864 | tf_op jit(solution)/shard_map/all_to_all | solution.py:44
  60.2 0.4 fusion.18
  60.7 1.6 copy.31
  62.3 21.6 %reduce-scatter.7.cloned.1.call-done = f32[384,4,128]{2,0,1:T(8,128)} async-done(((f32[768,4,128]{2,0,1:T(8,128)}), f32[384,4,128]{2,0,1:T(8,128)}) %reduce-scatter.7.cloned.1.call-update) | async-done | bytes 786448 | tf_op jit(solution)/shard_map/reduce_scatter | solution.py:68
  84.0 0.7 fusion.36
  84.6 62.3 %reduce-scatter.9.cloned.1.call-done = f32[32,4,128]{2,0,1:T(8,128)} async-done(((f32[384,4,128]{2,0,1:T(8,128)}), f32[32,4,128]{2,0,1:T(8,128)}) %reduce-scatter.9.cloned.1.call-update) | async-done | bytes 65552 | tf_op jit(solution)/shard_map/reduce_scatter | solution.py:68
  146.9 0.0 reduce-scatter.5.cloned.1.call-start
  147.0 2.7 %bitcast_convert_fusion = bf16[32,128,128]{2,0,1:T(8,128)(2,1)S(1)} fusion(f32[4,6,128,128]{3,2,1,0:T(8,128)S(1)} %fusion.36, s32[4,6]{1,0:T(4,128)S(1)} %reshape.87, pred[4,6]{1,0:T(4,128)(4,1)S(1)} %ge.24), kind=kOutput, calls=%fused_computation.17 | convolution fusion | flops 151520768 | bytes 2621560 | tf_op jit(solution)/shard_map/mctk,mcr->trk/dot_general | solution.py:52
  149.7 1.4 copy.57
  151.1 1.3 dynamic-slice
  153.1 77.0 %all-reduce.3.cloned.1.call-done = f32[32,4,128]{2,0,1:T(8,128)} async-done(((f32[32,4,128]{2,0,1:T(8,128)}), f32[32,4,128]{2,0,1:T(8,128)}) %all-reduce.3.cloned.1.call-update) | async-done | bytes 65552
  230.1 1.3 dynamic-slice_bitcast_fusion
  (18 shorter events, 0.2 us)
Async XLA Ops:
  8.0 20.8 %copy-start = (bf16[24,128,128]{2,1,0:T(8,128)(2,1)S(1)}, bf16[24,128,128]{2,1,0:T(8,128)(2,1)}, u32[]{:S(2)}) copy-start(bf16[24,128,128]{2,1,0:T(8,128)(2,1)} %param.6) | copy-start | bytes 2359300
  9.4 20.8 %all-to-all-start = ((s32[4,1,6]{2,1,0:T(1,128)}), s32[4,1,6]{2,1,0:T(1,128)S(1)}, u32[]{:S(2)}, u32[]{:S(2)}) async-start(s32[4,1,6]{2,1,0:T(1,128)} %bitcast), calls=%async_computation | async-start | bytes 4096 | tf_op jit(solution)/shard_map/all_to_all | solution.py:31
  30.2 14.0 %copy-start.1 = (bf16[128,4096]{1,0:T(8,128)(2,1)S(1)}, bf16[128,4096]{1,0:T(8,128)(2,1)}, u32[]{:S(2)}) copy-start(bf16[128,4096]{1,0:T(8,128)(2,1)} %param.9) | copy-start | bytes 3145732
  30.2 13.0 %all-to-all-start.1 = ((bf16[4,6,128,128]{3,2,1,0:T(8,128)(2,1)}), bf16[4,6,128,128]{3,2,1,0:T(8,128)(2,1)S(1)}, u32[]{:S(2)}, u32[]{:S(2)}) async-start(bf16[4,6,128,128]{3,2,1,0:T(8,128)(2,1)} %multiply_convert_fusion), calls=%async_computation.1 | async-start | bytes 1572864 | tf_op jit(solution)/shard_map/all_to_all | solution.py:30
  35.1 48.8 %reduce-scatter.7.cloned.1.call-start = ((), (), s32[]{:S(2)}) async-start(), calls=%async_computation.7 | async-start | bytes 2359296 | tf_op jit(solution)/shard_map/reduce_scatter | solution.py:68
  62.3 84.6 %reduce-scatter.9.cloned.1.call-start = ((), (), s32[]{:S(2)}) async-start(), calls=%async_computation.8 | async-start | bytes 851968 | tf_op jit(solution)/shard_map/reduce_scatter | solution.py:68
  83.9 146.2 %all-reduce.3.cloned.1.call-start = ((), (), s32[]{:S(2)}) async-start(), calls=%async_computation.9 | async-start | bytes 131072
  146.9 84.5 %reduce-scatter.5.cloned.1.call-start = ((), (), s32[]{:S(2)}) async-start(), calls=%async_computation.6 | async-start | bytes 1310720 | tf_op jit(solution)/shard_map/reduce_scatter | solution.py:56
Sparse Core Ops, SparseCore 0:
  62.4 21.4 reduce-scatter.6
  87.0 59.8 reduce-scatter.8
  149.2 80.8 all-reduce.2
Sparse Core Ops, SparseCore 1:
  151.2 27.8 reduce-scatter.4

commit v2 on v1

--- a/solution.py
+++ b/solution.py
@@ -63,9 +63,10 @@
     ny, nz, nc = lax.axis_size("y"), lax.axis_size("z"), lax.axis_size("c")
     rows = slot_cap * block_size // (ny * nz * nc)
     staged = weight_terms.reshape(mp_count, ny, nz, nc, rows, block_size)
-    staged = jnp.transpose(staged, (3, 2, 1, 4, 0, 5)).reshape(-1, mp_count, block_size)
-    for axis in ("c", "z", "y"):
-        staged = lax.psum_scatter(staged, axis, scatter_dimension=0, tiled=True)
+    staged = jnp.transpose(staged, (3, 1, 2, 4, 0, 5)).reshape(nc, -1, mp_count, block_size)
+    staged = lax.all_to_all(staged, "c", 0, 0, tiled=True).sum(0)
+    staged = staged.reshape(ny * nz, rows, mp_count, block_size)
+    staged = lax.all_to_all(staged, ("y", "z"), 0, 0, tiled=True).sum(0)
     summed = jnp.transpose(staged, (1, 0, 2))
     return (activation, input_grad, summed)
 

time: 239 us -> 131 us (0.55)
  the two profiles are of different devices: /device:TPU:2 before, /device:TPU:8 now
where the time goes in v2:
time: 131 us; the launch traced here: 130 us
  waiting for transfers between devices  42.5 us (32%)
  starting transfers between devices  31 us (24%)
  blocking collectives  18.3 us (14%)
  between operations  14.2 us (11%)
  local copies, waits for them, and re-layouts  11 us (8%)
  matrix products  6.7 us (5%)
  other arithmetic  6.42 us (5%)
    all_to_all x1, waiting for transfers between devices, body(): staged = lax.all_to_all(staged, ('y', 'z'), 0, 0, tiled=True).sum(0)  30.7 us
    all_to_all x1, starting transfers between devices, body(): staged = lax.all_to_all(staged, ('y', 'z'), 0, 0, tiled=True).sum(0)  21.8 us
    all_to_all x1, blocking collectives, body(): lax.all_to_all(returned, 'mp', split_axis=0, concat_axis=0, tiled=True)  13.3 us
    all_to_all x1, waiting for transfers between devices, body(): lax.all_to_all(own_parts, 'mp', split_axis=0, concat_axis=0, tiled=True)  11.7 us
    all_to_all x1, blocking collectives, body(): staged = lax.all_to_all(staged, 'c', 0, 0, tiled=True).sum(0)  5 us
    all_to_all x1, starting transfers between devices, body(): lax.all_to_all(own_parts, 'mp', split_axis=0, concat_axis=0, tiled=True)  4.93 us
    all_to_all x1, starting transfers between devices, body(): lax.all_to_all(col_groups, 'mp', split_axis=0, concat_axis=0, tiled=True)  4.29 us
    unnamed x7, local copies, waits for them, and re-layouts  3.93 us
  transfers between devices with their start and end apart: 4, of which 2 were waited for; matrix products, arithmetic and copies ran while one was open for 10% of the time, Pallas kernels for 0%

profile of v2, /device:TPU:8, one launch (start us, length us, event | category | flops | bytes accessed | tf_op | source)
XLA Modules:
  0.0 130.0 jit_solution(8533213112039339053)
XLA Ops:
  7.2 1.4 %all_to_all.18 = s32[4,1,6]{2,0,1:T(4,128)} reshape(s32[24]{0:T(128)} %param.8) | data formatting | bytes 192 | tf_op jit(solution)/shard_map/all_to_all | solution.py:31
  8.6 4.3 %all-to-all-start = ((s32[4,1,6]{2,1,0:T(1,128)}), s32[4,1,6]{2,1,0:T(1,128)S(1)}, u32[]{:S(2)}, u32[]{:S(2)}) async-start(s32[4,1,6]{2,1,0:T(1,128)} %bitcast), calls=%async_computation | async-start | bytes 4096 | tf_op jit(solution)/shard_map/all_to_all | solution.py:31
  12.9 0.7 broadcast_compare_fusion
  13.5 0.7 broadcast_maximum_fusion
  14.2 0.1 reshape.90
  14.3 0.1 reshape.92
  14.3 0.1 ge.24
  14.4 0.1 reshape.100
  14.5 2.3 %copy.32 = bf16[128,4096]{0,1:T(8,128)(2,1)} copy(bf16[128,4096]{1,0:T(8,128)(2,1)} %param.5) | data formatting | bytes 2097152 | tf_op args[0]
  16.8 1.6 %copy.33 = bf16[128,32,128]{2,0,1:T(8,128)(2,1)S(1)} copy(bf16[128,32,128]{0,2,1:T(8,128)(2,1)} %bitcast.75) | data formatting | bytes 2097152 | tf_op jit(solution)/shard_map/reshape | solution.py:19
  18.4 0.7 gather_fusion
  19.1 0.4 copy.34
  19.5 1.4 %multiply_convert_fusion = bf16[4,6,128,128]{3,2,1,0:T(8,128)(2,1)} fusion(bf16[4,6,128,128]{3,2,1,0:T(8,128)(2,1)S(1)} %bitcast.66, f32[4,6]{1,0:T(4,128)S(1)} %convert_element_type.33, bf16[4,6,128,128]{2,3,1,0:T(8,128)(2,1)S(1)} %copy.34, pred[4,6]{1,0:T(4,128)(4,1)S(1)} %compare_and_fusion), kind=kOutput, calls=%fused_computation.20 | convolution fusion | flops 101842944 | bytes 2359416 | tf_op jit(solution)/shard_map/tmck,mckn->mctn/dot_general | solution.py:25
  20.9 4.9 %all-to-all-start.1 = ((bf16[4,6,128,128]{3,2,1,0:T(8,128)(2,1)}), bf16[4,6,128,128]{3,2,1,0:T(8,128)(2,1)S(1)}, u32[]{:S(2)}, u32[]{:S(2)}) async-start(bf16[4,6,128,128]{3,2,1,0:T(8,128)(2,1)} %multiply_convert_fusion), calls=%async_computation.1 | async-start | bytes 1572864 | tf_op jit(solution)/shard_map/all_to_all | solution.py:30
  25.9 11.7 %all-to-all-done.1 = bf16[4,6,128,128]{3,2,1,0:T(8,128)(2,1)S(1)} async-done(((bf16[4,6,128,128]{3,2,1,0:T(8,128)(2,1)}), bf16[4,6,128,128]{3,2,1,0:T(8,128)(2,1)S(1)}, u32[]{:S(2)}, u32[]{:S(2)}) %all-to-all-start.1) | async-done | bytes 786464 | tf_op jit(solution)/shard_map/all_to_all | solution.py:30
  37.6 1.0 fusion.15
  38.7 3.3 %fusion.17 = (bf16[16,8,32,128]{3,1,2,0:T(8,128)(2,1)S(1)}, bf16[128,4096]{1,0:T(8,128)(2,1)}) fusion(f32[16,8,32,128]{3,2,1,0:T(8,128)S(1)} %bitcast.68, bf16[128,4096]{1,0:T(8,128)(2,1)S(1)} %copy-done.1), kind=kLoop, calls=%fused_computation.25 | loop fusion | flops 12058624 | bytes 5242880
  41.9 0.2 copy.46
  42.2 0.4 convolution_convert_fusion
  42.6 0.2 copy.37
  42.8 13.3 %all_to_all.29 = bf16[4,6,128,128]{3,2,1,0:T(8,128)(2,1)S(1)} all-to-all(bf16[4,6,128,128]{3,2,1,0:T(8,128)(2,1)S(1)} %copy.37), channel_id=1, replica_groups=mesh['y'=8,'z'=12,'c'=2,'mp'=4] {'mp'}, dimensions={0} | all-to-all | bytes 1572864 | tf_op jit(solution)/shard_map/all_to_all | solution.py:44
  56.1 0.4 fusion.18
  56.5 0.3 copy.39
  56.8 5.0 %all_to_all.30 = f32[2,384,4,128]{3,1,2,0:T(8,128)S(1)} all-to-all(f32[2,384,4,128]{3,1,2,0:T(8,128)S(1)} %bitcast.69), channel_id=1, replica_groups=mesh['y'=8,'z'=12,'c'=2,'mp'=4] {'c'}, dimensions={0} | all-to-all | bytes 3145728 | tf_op jit(solution)/shard_map/all_to_all | solution.py:67
  61.8 1.1 reduce_sum.18
  62.9 2.2 %copy.40 = f32[96,4,4,128]{3,1,2,0:T(4,128)} copy(f32[96,4,4,128]{3,1,0,2:T(4,128)} %bitcast.76) | data formatting | bytes 1572864 | tf_op jit(solution)/shard_map/reshape | solution.py:68
  65.0 21.8 %all-to-all-start.4 = ((f32[96,4,4,128]{3,1,2,0:T(4,128)}), f32[96,4,4,128]{3,1,2,0:T(4,128)S(1)}, u32[]{:S(2)}, u32[]{:S(2)}) async-start(f32[96,4,4,128]{3,1,2,0:T(4,128)} %copy.40), calls=%async_computation.5 | async-start | bytes 1572864 | tf_op jit(solution)/shard_map/all_to_all | solution.py:69
  86.9 0.7 fusion.36
  87.5 2.7 %bitcast_convert_fusion = bf16[32,128,128]{2,0,1:T(8,128)(2,1)S(1)} fusion(f32[4,6,128,128]{3,2,1,0:T(8,128)S(1)} %fusion.36, s32[4,6]{1,0:T(4,128)S(1)} %reshape.90, pred[4,6]{1,0:T(4,128)(4,1)S(1)} %ge.24), kind=kOutput, calls=%fused_computation.17 | convolution fusion | flops 151520768 | bytes 2621560 | tf_op jit(solution)/shard_map/mctk,mcr->trk/dot_general | solution.py:52
  90.3 1.4 %copy.64 = bf16[16,8,32,128]{3,1,2,0:T(8,128)(2,1)} copy(bf16[16,8,32,128]{3,2,1,0:T(8,128)(2,1)S(1)} %bitcast.72) | data formatting | bytes 2097152
  91.7 30.7 %all-to-all-done.4 = f32[96,4,4,128]{3,1,2,0:T(4,128)S(1)} async-done(((f32[96,4,4,128]{3,1,2,0:T(4,128)}), f32[96,4,4,128]{3,1,2,0:T(4,128)S(1)}, u32[]{:S(2)}, u32[]{:S(2)}) %all-to-all-start.4) | async-done | bytes 786464 | tf_op jit(solution)/shard_map/all_to_all | solution.py:69
  122.4 0.8 reduce_sum.19
  (13 shorter events, 0.1 us)
Async XLA Ops:
  7.2 12.4 %copy-start = (bf16[24,128,128]{2,1,0:T(8,128)(2,1)S(1)}, bf16[24,128,128]{2,1,0:T(8,128)(2,1)}, u32[]{:S(2)}) copy-start(bf16[24,128,128]{2,1,0:T(8,128)(2,1)} %param.6) | copy-start | bytes 2359300
  8.6 12.4 %all-to-all-start = ((s32[4,1,6]{2,1,0:T(1,128)}), s32[4,1,6]{2,1,0:T(1,128)S(1)}, u32[]{:S(2)}, u32[]{:S(2)}) async-start(s32[4,1,6]{2,1,0:T(1,128)} %bitcast), calls=%async_computation | async-start | bytes 4096 | tf_op jit(solution)/shard_map/all_to_all | solution.py:31
  20.9 17.7 %copy-start.1 = (bf16[128,4096]{1,0:T(8,128)(2,1)S(1)}, bf16[128,4096]{1,0:T(8,128)(2,1)}, u32[]{:S(2)}) copy-start(bf16[128,4096]{1,0:T(8,128)(2,1)} %param.9) | copy-start | bytes 3145732
  20.9 16.7 %all-to-all-start.1 = ((bf16[4,6,128,128]{3,2,1,0:T(8,128)(2,1)}), bf16[4,6,128,128]{3,2,1,0:T(8,128)(2,1)S(1)}, u32[]{:S(2)}, u32[]{:S(2)}) async-start(bf16[4,6,128,128]{3,2,1,0:T(8,128)(2,1)} %multiply_convert_fusion), calls=%async_computation.1 | async-start | bytes 1572864 | tf_op jit(solution)/shard_map/all_to_all | solution.py:30
  65.0 57.4 %all-to-all-start.4 = ((f32[96,4,4,128]{3,1,2,0:T(4,128)}), f32[96,4,4,128]{3,1,2,0:T(4,128)S(1)}, u32[]{:S(2)}, u32[]{:S(2)}) async-start(f32[96,4,4,128]{3,1,2,0:T(4,128)} %copy.40), calls=%async_computation.5 | async-start | bytes 1572864 | tf_op jit(solution)/shard_map/all_to_all | solution.py:69
  86.8 36.4 %reduce-scatter.2.cloned.1.call-start = ((), (), s32[]{:S(2)}) async-start(), calls=%async_computation.6 | async-start | bytes 1310720 | tf_op jit(solution)/shard_map/reduce_scatter | solution.py:56
Sparse Core Ops, SparseCore 0:
  91.8 30.3 reduce-scatter.1

commit v3 on v2

v3 whole, which is shorter than its diff:
```python
import jax
import jax.numpy as jnp
from jax import lax
from jax.sharding import Mesh, PartitionSpec as P


def gelu_tanh(inputs):
    return jax.nn.gelu(inputs, approximate=True)


def body(tokens, blocks, block_row, block_col, cotangent):
    mp_count = lax.axis_size("mp")
    token_count = tokens.shape[0]
    block_size = blocks.shape[1]
    row_blocks = tokens.shape[1] // block_size
    slot_cap = blocks.shape[0] // mp_count
    col_blocks = cotangent.shape[1] // block_size
    column_here = lax.axis_index("mp")
    w_groups = blocks.reshape(mp_count, slot_cap, block_size, block_size)
    w_here = lax.all_to_all(w_groups, "mp", 0, 0, tiled=True)
    lists = jnp.stack([block_row, block_col]).reshape(2, mp_count, slot_cap)
    lists = lax.all_to_all(lists, "mp", 1, 1, tiled=True)
    row_groups = jnp.maximum(lists[0], 0)
    col_groups = lists[1]
    slot_live = col_groups >= 0
    spread = tokens.reshape(token_count, row_blocks, block_size)
    picked_x = jnp.take(spread, row_groups, axis=1)
    live_mask = slot_live.astype(jnp.float32)
    parts = jnp.einsum(
        "tmck,mckn->mctn", picked_x, w_here, preferred_element_type=jnp.float32
    )
    parts = (parts * live_mask[:, :, None, None]).astype(jnp.bfloat16)
    local_col = col_groups - column_here * col_blocks
    onehot = (local_col[:, :, None] == jnp.arange(col_blocks)[None, None, :]).astype(jnp.bfloat16)
    pre_act = jnp.einsum("mctn,mcj->tjn", parts, onehot, preferred_element_type=jnp.float32)
    pre_act = pre_act.reshape(token_count, col_blocks * block_size)
    activation_f, pullback = jax.vjp(gelu_tanh, pre_act)
    activation = activation_f.astype(jnp.bfloat16)
    pre_grad = pullback(cotangent.astype(jnp.float32))[0].astype(jnp.bfloat16)
    pre_grad = pre_grad.reshape(token_count, col_blocks, block_size)
    grad_cols = jnp.einsum(
        "tjn,mcj->mctn", pre_grad, onehot, preferred_element_type=jnp.float32
    ).astype(jnp.bfloat16)
    input_terms = jnp.einsum(
        "mctn,mckn->mctk", grad_cols, w_here, preferred_element_type=jnp.float32
    )
    row_onehot = (
        (row_groups[:, :, None] == jnp.arange(row_blocks)[None, None, :]) & slot_live[:, :, None]
    ).astype(jnp.float32)
    input_partial = jnp.einsum(
        "mctk,mcr->trk", input_terms, row_onehot, precision=lax.Precision.HIGHEST
    )
    input_partial = input_partial.reshape(token_count, mp_count, row_blocks * block_size // mp_count)
    input_partial = lax.all_to_all(input_partial, "mp", 1, 1, tiled=True)
    input_grad = input_partial.sum(1).astype(jnp.bfloat16)
    weight_terms = jnp.einsum(
        "tmck,mctn->mckn", picked_x, grad_cols, preferred_element_type=jnp.float32
    )
    weight_terms = weight_terms.reshape(mp_count, slot_cap * block_size, block_size)
    ny, nz, nc = lax.axis_size("y"), lax.axis_size("z"), lax.axis_size("c")
    rows = slot_cap * block_size // (ny * nz * nc)
    staged = weight_terms.reshape(mp_count, ny, nz, nc, rows, block_size)
    staged = jnp.transpose(staged, (3, 1, 2, 4, 0, 5)).reshape(nc, -1, mp_count, block_size)
    staged = lax.all_to_all(staged, "c", 0, 0, tiled=True).sum(0)
    staged = staged.reshape(ny * nz, rows, mp_count, block_size)
    staged = lax.all_to_all(staged, ("y", "z"), 0, 0, tiled=True).sum(0)
    staged = lax.all_to_all(staged, "mp", 1, 1, tiled=True)
    summed = jnp.transpose(staged, (1, 0, 2))
    return (activation, input_grad, summed)


def solution(mesh):
    dp_count, mp_count = mesh.devices.shape
    y_count = len({d.coords[1] for d in mesh.devices.flat})
    chip_cores = len({d.core_on_chip for d in mesh.devices.flat})
    grid = mesh.devices.reshape(y_count, dp_count // (y_count * chip_cores), chip_cores, mp_count)
    split = Mesh(grid, ("y", "z", "c", "mp"))
    dp = ("y", "z", "c")
    placed = (P(dp, None), P("mp", None, None), P("mp"), P("mp"), P(dp, "mp"))
    return jax.shard_map(
        body,
        mesh=split,
        in_specs=placed,
        out_specs=(P(dp, "mp"), P(dp, "mp"), P("mp", dp, None)),
        check_vma=False,
    )
```

time: 131 us -> 134 us (1.023)
  waiting for transfers between devices: 42.5 us -> 66.9 us
  between operations: 14.2 us -> 0.82 us
  blocking collectives: 18.3 us -> 5 us
  starting transfers between devices: 31 us -> 36.4 us
  local copies, waits for them, and re-layouts: 11 us -> 13.7 us
    all_to_all x2 -> x4, waiting for transfers between devices: 11.7 us -> 40.5 us  [the longest x1 23.3 us: body(): input_partial = lax.all_to_all(input_partial, 'mp', 1, 1, tiled=True)]
    all_to_all x1 -> x0, blocking collectives: 13.3 us -> none  [body(): lax.all_to_all(returned, 'mp', split_axis=0, concat_axis=0, tiled=True)]
    reshape x2, local copies, waits for them, and re-layouts: 0.17 us -> 5.87 us  [body(): input_partial.reshape(token_count, mp_count, row_blocks * block_size // m...]
    all_to_all x2 -> x4, starting transfers between devices: 9.22 us -> 14.6 us  [the longest x1 4.29 us: body(): lists = lax.all_to_all(lists, 'mp', 1, 1, tiled=True)]
    all_to_all x1, waiting for transfers between devices: 30.7 us -> 26.4 us  [body(): staged = lax.all_to_all(staged, ('y', 'z'), 0, 0, tiled=True).sum(0)]
    another operation x0 -> x3, local copies, waits for them, and re-layouts: none -> 2.07 us  [body(): lists = jnp.stack([block_row, block_col]).reshape(2, mp_count, slot_cap)]
    all_to_all x1 -> x0, local copies, waits for them, and re-layouts: 1.39 us -> none  [body(): lax.all_to_all(col_groups, 'mp', split_axis=0, concat_axis=0, tiled=True)]
    unnamed x7 -> x9, local copies, waits for them, and re-layouts: 3.93 us -> 2.6 us
  transfers between devices with their start and end apart: 4 -> 5, of which waited for: 2 -> 5; matrix products, arithmetic and copies ran while one was open for 10% -> 11% of each run, Pallas kernels for 0% -> 0%
where the time goes in v3:
time: 134 us
  waiting for transfers between devices  66.9 us (50%)
  starting transfers between devices  36.4 us (27%)
  local copies, waits for them, and re-layouts  13.7 us (10%)
  matrix products  5.78 us (4%)
  other arithmetic  5.13 us (4%)
  blocking collectives  5 us (4%)
    all_to_all x1, waiting for transfers between devices, body(): staged = lax.all_to_all(staged, ('y', 'z'), 0, 0, tiled=True).sum(0)  26.4 us
    all_to_all x1, waiting for transfers between devices, body(): input_partial = lax.all_to_all(input_partial, 'mp', 1, 1, tiled=True)  23.3 us
    all_to_all x1, starting transfers between devices, body(): staged = lax.all_to_all(staged, ('y', 'z'), 0, 0, tiled=True).sum(0)  21.8 us
    all_to_all x1, waiting for transfers between devices, body(): w_here = lax.all_to_all(w_groups, 'mp', 0, 0, tiled=True)  9.85 us
    reshape x2, local copies, waits for them, and re-layouts, body(): input_partial.reshape(token_count, mp_count, row_blocks * block_size // m...  5.87 us
    all_to_all x1, blocking collectives, body(): staged = lax.all_to_all(staged, 'c', 0, 0, tiled=True).sum(0)  5 us
    all_to_all x1, waiting for transfers between devices, body(): staged = lax.all_to_all(staged, 'mp', 1, 1, tiled=True)  4.37 us
    all_to_all x1, starting transfers between devices, body(): lists = lax.all_to_all(lists, 'mp', 1, 1, tiled=True)  4.29 us
  transfers between devices with their start and end apart: 5, of which 5 were waited for; matrix products, arithmetic and copies ran while one was open for 11% of the time, Pallas kernels for 0%

profile of v3, /device:TPU:8, one launch (start us, length us, event | category | flops | bytes accessed | tf_op | source)
XLA Modules:
  0.0 133.8 jit_solution(15887840803426422719)
XLA Ops:
  0.6 0.7 stack.9
  1.4 0.7 stack.10
  2.1 0.6 copy.56
  2.7 4.3 %all-to-all-start = ((s32[2,4,6]{2,0,1:T(2,128)}), s32[2,4,6]{2,0,1:T(2,128)S(1)}, u32[]{:S(2)}, u32[]{:S(2)}) async-start(s32[2,4,6]{2,0,1:T(2,128)} %copy.56), calls=%async_computation | async-start | bytes 8192 | tf_op jit(solution)/shard_map/all_to_all | solution.py:22
  7.0 1.6 %copy.57 = bf16[128,4096]{0,1:T(8,128)(2,1)S(1)} copy(bf16[128,4096]{1,0:T(8,128)(2,1)} %param.5) | data formatting | bytes 2097152 | tf_op args[0]
  8.6 0.7 copy.58
  9.3 3.0 %all-to-all-done = s32[2,4,6]{2,0,1:T(2,128)S(1)} async-done(((s32[2,4,6]{2,0,1:T(2,128)}), s32[2,4,6]{2,0,1:T(2,128)S(1)}, u32[]{:S(2)}, u32[]{:S(2)}) %all-to-all-start) | async-done | bytes 224 | tf_op jit(solution)/shard_map/all_to_all | solution.py:22
  12.3 3.5 %all-to-all-start.1 = ((bf16[4,6,128,128]{3,2,1,0:T(8,128)(2,1)}), bf16[4,6,128,128]{3,2,1,0:T(8,128)(2,1)S(1)}, u32[]{:S(2)}, u32[]{:S(2)}) async-start(bf16[4,6,128,128]{3,2,1,0:T(8,128)(2,1)} %bitcast.6), calls=%async_computation.1 | async-start | bytes 1572864 | tf_op jit(solution)/shard_map/all_to_all | solution.py:20
  15.9 0.7 gather_fusion
  16.6 0.4 copy.59
  17.1 9.8 %all-to-all-done.1 = bf16[4,6,128,128]{3,2,1,0:T(8,128)(2,1)S(1)} async-done(((bf16[4,6,128,128]{3,2,1,0:T(8,128)(2,1)}), bf16[4,6,128,128]{3,2,1,0:T(8,128)(2,1)S(1)}, u32[]{:S(2)}, u32[]{:S(2)}) %all-to-all-start.1) | async-done | bytes 786464 | tf_op jit(solution)/shard_map/all_to_all | solution.py:20
  26.9 0.5 multiply_convert_fusion
  27.4 1.1 fusion.16
  28.7 3.2 %fusion.18 = (bf16[16,8,32,128]{3,1,2,0:T(8,128)(2,1)S(1)}, bf16[128,4096]{1,0:T(8,128)(2,1)}) fusion(f32[16,8,32,128]{3,2,1,0:T(8,128)S(1)} %bitcast.62, bf16[128,4096]{1,0:T(8,128)(2,1)S(1)} %copy-done.2), kind=kLoop, calls=%fused_computation.24 | loop fusion | flops 12058624 | bytes 5242880
  32.2 0.4 fusion.28
  32.6 0.4 fusion.19
  33.0 0.3 copy.65
  33.3 5.0 %all_to_all.30 = f32[2,384,4,128]{3,1,2,0:T(8,128)S(1)} all-to-all(f32[2,384,4,128]{3,1,2,0:T(8,128)S(1)} %bitcast.63), channel_id=1, replica_groups=mesh['y'=8,'z'=12,'c'=2,'mp'=4] {'c'}, dimensions={0} | all-to-all | bytes 3145728 | tf_op jit(solution)/shard_map/all_to_all | solution.py:64
  38.5 1.0 copy.66
  39.5 21.8 %all-to-all-start.4 = ((f32[96,4,4,128]{3,1,2,0:T(4,128)}), f32[96,4,4,128]{3,1,2,0:T(4,128)S(1)}, u32[]{:S(2)}, u32[]{:S(2)}) async-start(f32[96,4,4,128]{3,1,2,0:T(4,128)} %copy.66), calls=%async_computation.4 | async-start | bytes 1572864 | tf_op jit(solution)/shard_map/all_to_all | solution.py:66
  61.3 0.7 fusion.24
  62.0 2.7 %fusion.13 = f32[128,32,128]{2,1,0:T(8,128)S(1)} fusion(f32[4,6,128,128]{3,2,1,0:T(8,128)S(1)} %fusion.24, s32[4,6]{1,0:T(4,128)S(1)} %bitcast.71, pred[4,6]{1,0:T(4,128)(4,1)S(1)} %get-tuple-element.4), kind=kOutput, calls=%fused_computation.19 | convolution fusion | flops 150996480 | bytes 3670136 | tf_op jit(solution)/shard_map/mctk,mcr->trk/dot_general | solution.py:50
  64.7 1.7 %reshape.78 = f32[128,4,1024]{2,1,0:T(4,128)} reshape(f32[128,32,128]{2,1,0:T(8,128)S(1)} %fusion.13) | data formatting | bytes 4194304 | tf_op jit(solution)/shard_map/reshape | solution.py:53
  66.4 4.1 %copy.64 = f32[128,4,1024]{2,0,1:T(8,128)} copy(f32[128,4,1024]{2,1,0:T(4,128)} %reshape.78) | data formatting | bytes 4194304 | tf_op jit(solution)/shard_map/reshape | solution.py:53
  70.6 26.4 %all-to-all-done.4 = f32[96,4,4,128]{3,1,2,0:T(4,128)S(1)} async-done(((f32[96,4,4,128]{3,1,2,0:T(4,128)}), f32[96,4,4,128]{3,1,2,0:T(4,128)S(1)}, u32[]{:S(2)}, u32[]{:S(2)}) %all-to-all-start.4) | async-done | bytes 786464 | tf_op jit(solution)/shard_map/all_to_all | solution.py:66
  96.9 3.6 %all-to-all-start.2 = ((f32[128,4,1024]{2,0,1:T(8,128)}), f32[128,4,1024]{2,0,1:T(8,128)S(1)}, u32[]{:S(2)}, u32[]{:S(2)}) async-start(f32[128,4,1024]{2,0,1:T(8,128)} %copy.64), calls=%async_computation.2 | async-start | bytes 4194304 | tf_op jit(solution)/shard_map/all_to_all | solution.py:54
  100.5 0.8 reduce_sum.29
  101.3 23.3 %all-to-all-done.2 = f32[128,4,1024]{2,0,1:T(8,128)S(1)} async-done(((f32[128,4,1024]{2,0,1:T(8,128)}), f32[128,4,1024]{2,0,1:T(8,128)S(1)}, u32[]{:S(2)}, u32[]{:S(2)}) %all-to-all-start.2) | async-done | bytes 2097184 | tf_op jit(solution)/shard_map/all_to_all | solution.py:54
  124.6 3.2 %all-to-all-start.5 = ((f32[4,4,128]{2,0,1:T(4,128)}), f32[4,4,128]{2,0,1:T(4,128)S(1)}, u32[]{:S(2)}, u32[]{:S(2)}) async-start(f32[4,4,128]{2,0,1:T(4,128)} %reduce_sum.29), calls=%async_computation.5 | async-start | bytes 16384 | tf_op jit(solution)/shard_map/all_to_all | solution.py:67
  127.9 0.9 reduce_sum.27
  128.8 4.4 %all-to-all-done.5 = f32[4,4,128]{2,0,1:T(4,128)S(1)} async-done(((f32[4,4,128]{2,0,1:T(4,128)}), f32[4,4,128]{2,0,1:T(4,128)S(1)}, u32[]{:S(2)}, u32[]{:S(2)}) %all-to-all-start.5) | async-done | bytes 8224 | tf_op jit(solution)/shard_map/all_to_all | solution.py:67
  133.2 0.6 copy.95
  (15 shorter events, 0.7 us)
Async XLA Ops:
  2.7 9.6 %all-to-all-start = ((s32[2,4,6]{2,0,1:T(2,128)}), s32[2,4,6]{2,0,1:T(2,128)S(1)}, u32[]{:S(2)}, u32[]{:S(2)}) async-start(s32[2,4,6]{2,0,1:T(2,128)} %copy.56), calls=%async_computation | async-start | bytes 8192 | tf_op jit(solution)/shard_map/all_to_all | solution.py:22
  12.3 14.6 %all-to-all-start.1 = ((bf16[4,6,128,128]{3,2,1,0:T(8,128)(2,1)}), bf16[4,6,128,128]{3,2,1,0:T(8,128)(2,1)S(1)}, u32[]{:S(2)}, u32[]{:S(2)}) async-start(bf16[4,6,128,128]{3,2,1,0:T(8,128)(2,1)} %bitcast.6), calls=%async_computation.1 | async-start | bytes 1572864 | tf_op jit(solution)/shard_map/all_to_all | solution.py:20
  26.9 1.6 %copy-start = (bf16[4,6,128,128]{3,2,1,0:T(8,128)(2,1)}, bf16[4,6,128,128]{3,2,1,0:T(8,128)(2,1)S(1)}, u32[]{:S(2)}) copy-start(bf16[4,6,128,128]{3,2,1,0:T(8,128)(2,1)S(1)} %all-to-all-done.1) | copy-start | bytes 2359300
  27.4 1.2 copy-start.2
  38.5 22.8 %copy-start.1 = (bf16[4,6,128,128]{3,2,1,0:T(8,128)(2,1)S(1)}, bf16[4,6,128,128]{3,2,1,0:T(8,128)(2,1)}, u32[]{:S(2)}) copy-start(bf16[4,6,128,128]{3,2,1,0:T(8,128)(2,1)} %copy-done) | copy-start | bytes 2359300
  39.5 57.4 %all-to-all-start.4 = ((f32[96,4,4,128]{3,1,2,0:T(4,128)}), f32[96,4,4,128]{3,1,2,0:T(4,128)S(1)}, u32[]{:S(2)}, u32[]{:S(2)}) async-start(f32[96,4,4,128]{3,1,2,0:T(4,128)} %copy.66), calls=%async_computation.4 | async-start | bytes 1572864 | tf_op jit(solution)/shard_map/all_to_all | solution.py:66
  96.9 27.7 %all-to-all-start.2 = ((f32[128,4,1024]{2,0,1:T(8,128)}), f32[128,4,1024]{2,0,1:T(8,128)S(1)}, u32[]{:S(2)}, u32[]{:S(2)}) async-start(f32[128,4,1024]{2,0,1:T(8,128)} %copy.64), calls=%async_computation.2 | async-start | bytes 4194304 | tf_op jit(solution)/shard_map/all_to_all | solution.py:54
  124.6 8.5 %all-to-all-start.5 = ((f32[4,4,128]{2,0,1:T(4,128)}), f32[4,4,128]{2,0,1:T(4,128)S(1)}, u32[]{:S(2)}, u32[]{:S(2)}) async-start(f32[4,4,128]{2,0,1:T(4,128)} %reduce_sum.29), calls=%async_computation.5 | async-start | bytes 16384 | tf_op jit(solution)/shard_map/all_to_all | solution.py:67

commit v4 on v3

--- a/solution.py
+++ b/solution.py
@@ -16,12 +16,14 @@
     slot_cap = blocks.shape[0] // mp_count
     col_blocks = cotangent.shape[1] // block_size
     column_here = lax.axis_index("mp")
-    w_groups = blocks.reshape(mp_count, slot_cap, block_size, block_size)
-    w_here = lax.all_to_all(w_groups, "mp", 0, 0, tiled=True)
-    lists = jnp.stack([block_row, block_col]).reshape(2, mp_count, slot_cap)
-    lists = lax.all_to_all(lists, "mp", 1, 1, tiled=True)
-    row_groups = jnp.maximum(lists[0], 0)
-    col_groups = lists[1]
+    w_groups = blocks.reshape(mp_count, slot_cap * block_size, block_size)
+    lists = jnp.stack([block_row, block_col], 1).reshape(mp_count, 1, slot_cap * 2)
+    lists = jnp.pad(lists.astype(jnp.bfloat16), ((0, 0), (0, 15), (0, block_size - slot_cap * 2)))
+    sent = lax.all_to_all(jnp.concatenate([w_groups, lists], 1), "mp", 0, 0, tiled=True)
+    w_here = sent[:, : slot_cap * block_size].reshape(mp_count, slot_cap, block_size, block_size)
+    lists = sent[:, slot_cap * block_size, : slot_cap * 2].astype(jnp.int32).reshape(mp_count, slot_cap, 2)
+    row_groups = jnp.maximum(lists[:, :, 0], 0)
+    col_groups = lists[:, :, 1]
     slot_live = col_groups >= 0
     spread = tokens.reshape(token_count, row_blocks, block_size)
     picked_x = jnp.take(spread, row_groups, axis=1)
@@ -50,9 +52,9 @@
     input_partial = jnp.einsum(
         "mctk,mcr->trk", input_terms, row_onehot, precision=lax.Precision.HIGHEST
     )
-    input_partial = input_partial.reshape(token_count, mp_count, row_blocks * block_size // mp_count)
-    input_partial = lax.all_to_all(input_partial, "mp", 1, 1, tiled=True)
-    input_grad = input_partial.sum(1).astype(jnp.bfloat16)
+    input_partial = input_partial.reshape(token_count, row_blocks * block_size)
+    input_grad = lax.psum_scatter(input_partial, "mp", scatter_dimension=1, tiled=True)
+    input_grad = input_grad.astype(jnp.bfloat16)
     weight_terms = jnp.einsum(
         "tmck,mctn->mckn", picked_x, grad_cols, preferred_element_type=jnp.float32
     )

time: 134 us -> 124 us (0.925)
  blocking collectives: 5 us -> 69.8 us
  waiting for transfers between devices: 66.9 us -> 11.4 us
  starting transfers between devices: 36.4 us -> 4.29 us
  between operations: 0.82 us -> 14.1 us
  local copies, waits for them, and re-layouts: 13.7 us -> 9.33 us
  other arithmetic: 5.13 us -> 8.23 us
    all_to_all x0 -> x2, blocking collectives: none -> 64.8 us  [the longest x1 57.2 us: body(): staged = lax.all_to_all(staged, ('y', 'z'), 0, 0, tiled=True).sum(0)]
    all_to_all x5 -> x1, waiting for transfers between devices: 66.9 us -> 11.4 us  [body(): lax.all_to_all(jnp.concatenate([w_groups, lists], 1), 'mp', 0, 0, tiled=T...]
    all_to_all x5 -> x1, starting transfers between devices: 36.4 us -> 4.29 us  [body(): lax.all_to_all(jnp.concatenate([w_groups, lists], 1), 'mp', 0, 0, tiled=T...]
    reshape x2 -> x0, local copies, waits for them, and re-layouts: 5.87 us -> none  [body(): input_partial.reshape(token_count, mp_count, row_blocks * block_size // m...]
    unnamed x9 -> x10, local copies, waits for them, and re-layouts: 2.6 us -> 4.82 us
    concatenate x0 -> x1, other arithmetic: none -> 2.07 us  [body(): jnp.concatenate([w_groups, lists], 1)]
    slice x0 -> x3, local copies, waits for them, and re-layouts: none -> 1.98 us  [the longest x1 1.19 us: body(): sent[:, :slot_cap * block_size]]
    another operation x3 -> x1, local copies, waits for them, and re-layouts: 2.07 us -> 0.1 us  [body(): jnp.stack([block_row, block_col], 1).reshape(mp_count, 1, slot_cap * 2)]
  transfers between devices with their start and end apart: 5 -> 2, of which waited for: 5 -> 1; matrix products, arithmetic and copies ran while one was open for 11% -> 2% of each run, Pallas kernels for 0% -> 0%
where the time goes in v4:
time: 124 us; the launch traced here: 123 us
  blocking collectives  69.8 us (56%)
  between operations  14.1 us (11%)
  waiting for transfers between devices  11.4 us (9%)
  local copies, waits for them, and re-layouts  9.33 us (8%)
  other arithmetic  8.23 us (7%)
  matrix products  5.83 us (5%)
  starting transfers between devices  4.29 us (3%)
    all_to_all x1, blocking collectives, body(): staged = lax.all_to_all(staged, ('y', 'z'), 0, 0, tiled=True).sum(0)  57.2 us
    all_to_all x1, waiting for transfers between devices, body(): lax.all_to_all(jnp.concatenate([w_groups, lists], 1), 'mp', 0, 0, tiled=T...  11.4 us
    all_to_all x1, blocking collectives, body(): staged = lax.all_to_all(staged, 'mp', 1, 1, tiled=True)  7.65 us
    all_to_all x1, blocking collectives, body(): staged = lax.all_to_all(staged, 'c', 0, 0, tiled=True).sum(0)  5 us
    unnamed x10, local copies, waits for them, and re-layouts  4.82 us
    all_to_all x1, starting transfers between devices, body(): lax.all_to_all(jnp.concatenate([w_groups, lists], 1), 'mp', 0, 0, tiled=T...  4.29 us
    unnamed x1, other arithmetic  3.24 us
    dot_general x1, matrix products, body(): jnp.einsum('mctk,mcr->trk', input_terms, row_onehot, precision=lax.Precis...  2.71 us
  transfers between devices with their start and end apart: 2, of which 1 were waited for; matrix products, arithmetic and copies ran while one was open for 2% of the time, Pallas kernels for 0%

profile of v4, /device:TPU:8, one launch (start us, length us, event | category | flops | bytes accessed | tf_op | source)
XLA Modules:
  0.0 123.1 jit_solution(943338990708565651)
XLA Ops:
  7.2 0.8 convert_bitcast_fusion
  8.0 0.1 copy.82
  8.1 2.1 %fusion.17 = bf16[4,784,128]{2,1,0:T(8,128)(2,1)} fusion(bf16[4,1,12]{2,1,0:T(2,128)(2,1)S(1)} %convert_element_type.63, bf16[4,768,128]{2,1,0:T(8,128)(2,1)} %bitcast.89), kind=kLoop, calls=%fused_computation.27 | loop fusion | flops 2408448 | bytes 1589344 | tf_op jit(solution)/shard_map/concatenate | solution.py:22
  10.2 4.3 %all-to-all-start = ((bf16[4,784,128]{2,1,0:T(8,128)(2,1)}), bf16[4,784,128]{2,1,0:T(8,128)(2,1)}, u32[]{:S(2)}, u32[]{:S(2)}) async-start(bf16[4,784,128]{2,1,0:T(8,128)(2,1)} %fusion.17), calls=%async_computation | async-start | bytes 1605632 | tf_op jit(solution)/shard_map/all_to_all | solution.py:22
  14.5 0.7 copy.88
  15.2 0.7 copy.89
  15.9 11.4 %all-to-all-done = bf16[4,784,128]{2,1,0:T(8,128)(2,1)} async-done(((bf16[4,784,128]{2,1,0:T(8,128)(2,1)}), bf16[4,784,128]{2,1,0:T(8,128)(2,1)}, u32[]{:S(2)}, u32[]{:S(2)}) %all-to-all-start) | async-done | bytes 802848 | tf_op jit(solution)/shard_map/all_to_all | solution.py:22
  27.2 0.7 slice.18
  28.1 0.1 copy.105
  28.2 0.1 copy.104
  28.4 0.7 gather_fusion
  29.1 0.4 copy.90
  29.5 1.2 slice.21
  30.7 0.5 multiply_convert_fusion
  31.3 1.1 fusion.14
  32.4 0.1 copy-done
  32.5 3.2 %fusion.16 = (bf16[16,8,32,128]{3,1,2,0:T(8,128)(2,1)S(1)}, bf16[128,4096]{1,0:T(8,128)(2,1)}) fusion(f32[16,8,32,128]{3,2,1,0:T(8,128)S(1)} %bitcast.79, bf16[128,4096]{1,0:T(8,128)(2,1)S(1)} %copy-done), kind=kLoop, calls=%fused_computation.26 | loop fusion | flops 12058624 | bytes 5242880
  35.7 0.2 copy.108
  36.0 0.4 fusion.27
  36.4 0.7 fusion.23
  37.1 2.7 %fusion.11 = f32[32,128,128,1]{2,0,3,1:T(8,128)S(1)} fusion(f32[4,6,128,128]{3,2,1,0:T(8,128)S(1)} %fusion.23, s32[4,6]{1,0:T(4,128)S(1)} %get-tuple-element.9, pred[4,6]{1,0:T(4,128)(4,1)S(1)} %get-tuple-element.4), kind=kOutput, calls=%fused_computation.18 | convolution fusion | flops 150996480 | bytes 3670136 | tf_op jit(solution)/shard_map/mctk,mcr->trk/dot_general | solution.py:52
  39.8 3.0 %copy.128 = f32[16,8,32,128]{3,1,2,0:T(8,128)} copy(f32[16,8,32,128]{3,2,1,0:T(8,128)S(1)} %bitcast.80) | data formatting | bytes 4194304
  42.8 0.4 fusion.18
  43.2 0.3 copy.95
  43.5 5.0 %all_to_all.20 = f32[2,384,4,128]{3,1,2,0:T(8,128)S(1)} all-to-all(f32[2,384,4,128]{3,1,2,0:T(8,128)S(1)} %bitcast.81), channel_id=1, replica_groups=mesh['y'=8,'z'=12,'c'=2,'mp'=4] {'c'}, dimensions={0} | all-to-all | bytes 3145728 | tf_op jit(solution)/shard_map/all_to_all | solution.py:66
  48.5 0.2 reduce_sum.18
  48.7 0.1 copy.96
  48.8 57.2 %all_to_all.21 = f32[96,4,4,128]{3,1,2,0:T(4,128)S(1)} all-to-all(f32[96,4,4,128]{3,1,2,0:T(4,128)S(1)} %copy.96), channel_id=1, replica_groups=mesh['y'=8,'z'=12,'c'=2,'mp'=4] {'y','z'}, dimensions={0} | all-to-all | bytes 1572864 | tf_op jit(solution)/shard_map/all_to_all | solution.py:68
  106.0 0.2 reduce_sum.19
  106.2 7.6 %all_to_all.22 = f32[4,4,128]{2,0,1:T(4,128)S(1)} all-to-all(f32[4,4,128]{2,0,1:T(4,128)S(1)} %reduce_sum.19), channel_id=1, replica_groups=mesh['y'=8,'z'=12,'c'=2,'mp'=4] {'mp'}, dimensions={1} | all-to-all | bytes 16384 | tf_op jit(solution)/shard_map/all_to_all | solution.py:69
  113.8 1.8 %convert_element_type.61 = bf16[128,1024]{1,0:T(8,128)(2,1)} convert(f32[128,1024]{1,0:T(8,128)} %reduce-scatter.2.cloned.1.call-done) | non-fusion elementwise | flops 131072 | bytes 786432 | tf_op jit(solution)/shard_map/convert_element_type | solution.py:57
  115.6 0.6 copy.130
  (17 shorter events, 0.4 us)
Async XLA Ops:
  7.2 7.3 %copy-start.1 = (bf16[128,4096]{1,0:T(8,128)(2,1)S(1)}, bf16[128,4096]{1,0:T(8,128)(2,1)}, u32[]{:S(2)}) copy-start(bf16[128,4096]{1,0:T(8,128)(2,1)} %param.5) | copy-start | bytes 3145732
  10.2 17.0 %all-to-all-start = ((bf16[4,784,128]{2,1,0:T(8,128)(2,1)}), bf16[4,784,128]{2,1,0:T(8,128)(2,1)}, u32[]{:S(2)}, u32[]{:S(2)}) async-start(bf16[4,784,128]{2,1,0:T(8,128)(2,1)} %fusion.17), calls=%async_computation | async-start | bytes 1605632 | tf_op jit(solution)/shard_map/all_to_all | solution.py:22
  14.5 99.3 %reduce-scatter.2.cloned.1.call-start = ((), (), s32[]{:S(2)}) async-start(), calls=%async_computation.5 | async-start | bytes 2621440 | tf_op jit(solution)/shard_map/reduce_scatter | solution.py:56
  31.3 1.2 copy-start
Sparse Core Ops, SparseCore 0:
  42.9 42.5 reduce-scatter.1

commit v5 on v4

--- a/solution.py
+++ b/solution.py
@@ -65,7 +65,8 @@
     staged = jnp.transpose(staged, (3, 1, 2, 4, 0, 5)).reshape(nc, -1, mp_count, block_size)
     staged = lax.all_to_all(staged, "c", 0, 0, tiled=True).sum(0)
     staged = staged.reshape(ny * nz, rows, mp_count, block_size)
-    staged = lax.all_to_all(staged, ("y", "z"), 0, 0, tiled=True).sum(0)
+    staged = lax.all_to_all(staged.astype(jnp.bfloat16), ("y", "z"), 0, 0, tiled=True)
+    staged = staged.astype(jnp.float32).sum(0)
     staged = lax.all_to_all(staged, "mp", 1, 1, tiled=True)
     summed = jnp.transpose(staged, (1, 0, 2))
     return (activation, input_grad, summed)

time: 124 us -> 111 us (0.90)
  blocking collectives: 69.8 us -> 57.7 us
    all_to_all x1, blocking collectives: 57.2 us -> 45 us  [body(): lax.all_to_all(staged.astype(jnp.bfloat16), ('y', 'z'), 0, 0, tiled=True)]
where the time goes in v5:
time: 111 us
  blocking collectives  57.7 us (52%)
  between operations  14.1 us (13%)
  waiting for transfers between devices  11.4 us (10%)
  local copies, waits for them, and re-layouts  9.33 us (8%)
  other arithmetic  8.19 us (7%)
  matrix products  5.83 us (5%)
  starting transfers between devices  4.29 us (4%)
    all_to_all x1, blocking collectives, body(): lax.all_to_all(staged.astype(jnp.bfloat16), ('y', 'z'), 0, 0, tiled=True)  45 us
    all_to_all x1, waiting for transfers between devices, body(): lax.all_to_all(jnp.concatenate([w_groups, lists], 1), 'mp', 0, 0, tiled=T...  11.4 us
    all_to_all x1, blocking collectives, body(): staged = lax.all_to_all(staged, 'mp', 1, 1, tiled=True)  7.65 us
    all_to_all x1, blocking collectives, body(): staged = lax.all_to_all(staged, 'c', 0, 0, tiled=True).sum(0)  5 us
    unnamed x10, local copies, waits for them, and re-layouts  4.82 us
    all_to_all x1, starting transfers between devices, body(): lax.all_to_all(jnp.concatenate([w_groups, lists], 1), 'mp', 0, 0, tiled=T...  4.29 us
    unnamed x1, other arithmetic  3.24 us
    dot_general x1, matrix products, body(): jnp.einsum('mctk,mcr->trk', input_terms, row_onehot, precision=lax.Precis...  2.71 us
  transfers between devices with their start and end apart: 2, of which 1 were waited for; matrix products, arithmetic and copies ran while one was open for 2% of the time, Pallas kernels for 0%

profile of v5, /device:TPU:8, one launch (start us, length us, event | category | flops | bytes accessed | tf_op | source)
XLA Modules:
  0.0 110.8 jit_solution(14096189167091892056)
XLA Ops:
  7.2 0.8 convert_bitcast_fusion
  8.0 0.1 copy.82
  8.1 0.1 convert_element_type.75
  8.1 2.1 %fusion.17 = bf16[4,784,128]{2,1,0:T(8,128)(2,1)} fusion(bf16[4,1,12]{2,1,0:T(2,128)(2,1)S(1)} %convert_element_type.75, bf16[4,768,128]{2,1,0:T(8,128)(2,1)} %bitcast.89), kind=kLoop, calls=%fused_computation.27 | loop fusion | flops 2408448 | bytes 1589344 | tf_op jit(solution)/shard_map/concatenate | solution.py:22
  10.2 4.3 %all-to-all-start = ((bf16[4,784,128]{2,1,0:T(8,128)(2,1)}), bf16[4,784,128]{2,1,0:T(8,128)(2,1)}, u32[]{:S(2)}, u32[]{:S(2)}) async-start(bf16[4,784,128]{2,1,0:T(8,128)(2,1)} %fusion.17), calls=%async_computation | async-start | bytes 1605632 | tf_op jit(solution)/shard_map/all_to_all | solution.py:22
  14.5 0.7 copy.88
  15.2 0.7 copy.89
  15.9 11.4 %all-to-all-done = bf16[4,784,128]{2,1,0:T(8,128)(2,1)} async-done(((bf16[4,784,128]{2,1,0:T(8,128)(2,1)}), bf16[4,784,128]{2,1,0:T(8,128)(2,1)}, u32[]{:S(2)}, u32[]{:S(2)}) %all-to-all-start) | async-done | bytes 802848 | tf_op jit(solution)/shard_map/all_to_all | solution.py:22
  27.2 0.7 slice.18
  28.1 0.1 copy.105
  28.2 0.1 copy.104
  28.4 0.7 gather_fusion
  29.1 0.4 copy.90
  29.5 1.2 %slice.21 = bf16[4,768,128]{2,1,0:T(8,128)(2,1)S(1)} slice(bf16[4,784,128]{2,1,0:T(8,128)(2,1)} %all-to-all-done), slice={[0:4], [0:768], [0:128]} | slice | bytes 1572864 | tf_op jit(solution)/shard_map/slice | solution.py:23
  30.7 0.5 multiply_convert_fusion
  31.3 1.1 fusion.14
  32.4 0.1 copy-done
  32.5 3.2 %fusion.16 = (bf16[16,8,32,128]{3,1,2,0:T(8,128)(2,1)S(1)}, bf16[128,4096]{1,0:T(8,128)(2,1)}) fusion(f32[16,8,32,128]{3,2,1,0:T(8,128)S(1)} %bitcast.79, bf16[128,4096]{1,0:T(8,128)(2,1)S(1)} %copy-done), kind=kLoop, calls=%fused_computation.26 | loop fusion | flops 12058624 | bytes 5242880
  35.7 0.2 copy.108
  36.0 0.4 fusion.27
  36.4 0.7 fusion.23
  37.1 2.7 %fusion.11 = f32[32,128,128,1]{2,0,3,1:T(8,128)S(1)} fusion(f32[4,6,128,128]{3,2,1,0:T(8,128)S(1)} %fusion.23, s32[4,6]{1,0:T(4,128)S(1)} %get-tuple-element.9, pred[4,6]{1,0:T(4,128)(4,1)S(1)} %get-tuple-element.4), kind=kOutput, calls=%fused_computation.18 | convolution fusion | flops 150996480 | bytes 3670136 | tf_op jit(solution)/shard_map/mctk,mcr->trk/dot_general | solution.py:52
  39.8 3.0 %copy.128 = f32[16,8,32,128]{3,1,2,0:T(8,128)} copy(f32[16,8,32,128]{3,2,1,0:T(8,128)S(1)} %bitcast.80) | data formatting | bytes 4194304
  42.8 0.4 fusion.18
  43.2 0.3 copy.95
  43.5 5.0 %all_to_all.20 = f32[2,384,4,128]{3,1,2,0:T(8,128)S(1)} all-to-all(f32[2,384,4,128]{3,1,2,0:T(8,128)S(1)} %bitcast.81), channel_id=1, replica_groups=mesh['y'=8,'z'=12,'c'=2,'mp'=4] {'c'}, dimensions={0} | all-to-all | bytes 3145728 | tf_op jit(solution)/shard_map/all_to_all | solution.py:66
  48.6 0.1 copy.96
  48.7 45.0 %all_to_all.21 = bf16[96,4,4,128]{3,1,2,0:T(4,128)(2,1)S(1)} all-to-all(bf16[96,4,4,128]{3,1,2,0:T(4,128)(2,1)S(1)} %copy.96), channel_id=1, replica_groups=mesh['y'=8,'z'=12,'c'=2,'mp'=4] {'y','z'}, dimensions={0} | all-to-all | bytes 786432 | tf_op jit(solution)/shard_map/all_to_all | solution.py:68
  93.7 0.2 convert_reduce_fusion
  94.0 7.6 %all_to_all.22 = f32[4,4,128]{2,0,1:T(4,128)S(1)} all-to-all(f32[4,4,128]{2,0,1:T(4,128)S(1)} %convert_reduce_fusion), channel_id=1, replica_groups=mesh['y'=8,'z'=12,'c'=2,'mp'=4] {'mp'}, dimensions={1} | all-to-all | bytes 16384 | tf_op jit(solution)/shard_map/all_to_all | solution.py:70
  101.6 1.8 %convert_element_type.70 = bf16[128,1024]{1,0:T(8,128)(2,1)} convert(f32[128,1024]{1,0:T(8,128)} %reduce-scatter.2.cloned.1.call-done) | non-fusion elementwise | flops 131072 | bytes 786432 | tf_op jit(solution)/shard_map/convert_element_type | solution.py:57
  103.4 0.6 copy.130
  (17 shorter events, 0.4 us)
Async XLA Ops:
  7.2 7.3 %copy-start.1 = (bf16[128,4096]{1,0:T(8,128)(2,1)S(1)}, bf16[128,4096]{1,0:T(8,128)(2,1)}, u32[]{:S(2)}) copy-start(bf16[128,4096]{1,0:T(8,128)(2,1)} %param.5) | copy-start | bytes 3145732
  10.2 17.0 %all-to-all-start = ((bf16[4,784,128]{2,1,0:T(8,128)(2,1)}), bf16[4,784,128]{2,1,0:T(8,128)(2,1)}, u32[]{:S(2)}, u32[]{:S(2)}) async-start(bf16[4,784,128]{2,1,0:T(8,128)(2,1)} %fusion.17), calls=%async_computation | async-start | bytes 1605632 | tf_op jit(solution)/shard_map/all_to_all | solution.py:22
  14.5 87.1 %reduce-scatter.2.cloned.1.call-start = ((), (), s32[]{:S(2)}) async-start(), calls=%async_computation.5 | async-start | bytes 2621440 | tf_op jit(solution)/shard_map/reduce_scatter | solution.py:56
  31.3 1.2 %copy-start = (bf16[128,4096]{1,0:T(8,128)(2,1)S(1)}, bf16[128,4096]{1,0:T(8,128)(2,1)}, u32[]{:S(2)}) copy-start(bf16[128,4096]{1,0:T(8,128)(2,1)} %param.9) | copy-start | bytes 3145732
Sparse Core Ops, SparseCore 0:
  42.9 42.5 reduce-scatter.1

commit v6 on v5

--- a/solution.py
+++ b/solution.py
@@ -50,11 +50,11 @@
         (row_groups[:, :, None] == jnp.arange(row_blocks)[None, None, :]) & slot_live[:, :, None]
     ).astype(jnp.float32)
     input_partial = jnp.einsum(
-        "mctk,mcr->trk", input_terms, row_onehot, precision=lax.Precision.HIGHEST
+        "mctk,mcr->rtk", input_terms, row_onehot, precision=lax.Precision.HIGHEST
     )
-    input_partial = input_partial.reshape(token_count, row_blocks * block_size)
-    input_grad = lax.psum_scatter(input_partial, "mp", scatter_dimension=1, tiled=True)
-    input_grad = input_grad.astype(jnp.bfloat16)
+    input_grad = lax.psum_scatter(input_partial, "mp", scatter_dimension=0, tiled=True)
+    input_grad = jnp.transpose(input_grad.astype(jnp.bfloat16), (1, 0, 2))
+    input_grad = input_grad.reshape(token_count, row_blocks * block_size // mp_count)
     weight_terms = jnp.einsum(
         "tmck,mctn->mckn", picked_x, grad_cols, preferred_element_type=jnp.float32
     )

time: 111 us -> 110 us (level)
  local copies, waits for them, and re-layouts: 9.33 us -> 7.11 us
  matrix products: 5.83 us -> 7.14 us
    unnamed x10, local copies, waits for them, and re-layouts: 4.82 us -> 2.6 us
    dot_general x1, matrix products: 2.71 us -> 4.03 us  [body(): jnp.einsum('mctk,mcr->rtk', input_terms, row_onehot, precision=lax.Precis...]
where the time goes in v6:
time: 110 us; the launch traced here: 109 us
  blocking collectives  57.7 us (52%)
  between operations  14.1 us (13%)
  waiting for transfers between devices  11.4 us (10%)
  other arithmetic  7.48 us (7%)
  matrix products  7.14 us (6%)
  local copies, waits for them, and re-layouts  7.11 us (6%)
  starting transfers between devices  4.29 us (4%)
    all_to_all x1, blocking collectives, body(): lax.all_to_all(staged.astype(jnp.bfloat16), ('y', 'z'), 0, 0, tiled=True)  45 us
    all_to_all x1, waiting for transfers between devices, body(): lax.all_to_all(jnp.concatenate([w_groups, lists], 1), 'mp', 0, 0, tiled=T...  11.4 us
    all_to_all x1, blocking collectives, body(): staged = lax.all_to_all(staged, 'mp', 1, 1, tiled=True)  7.65 us
    all_to_all x1, blocking collectives, body(): staged = lax.all_to_all(staged, 'c', 0, 0, tiled=True).sum(0)  5 us
    all_to_all x1, starting transfers between devices, body(): lax.all_to_all(jnp.concatenate([w_groups, lists], 1), 'mp', 0, 0, tiled=T...  4.29 us
    dot_general x1, matrix products, body(): jnp.einsum('mctk,mcr->rtk', input_terms, row_onehot, precision=lax.Precis...  4.03 us
    unnamed x1, other arithmetic  3.24 us
    unnamed x10, local copies, waits for them, and re-layouts  2.6 us
  transfers between devices with their start and end apart: 2, of which 1 were waited for; matrix products, arithmetic and copies ran while one was open for 2% of the time, Pallas kernels for 0%

profile of v6, /device:TPU:8, one launch (start us, length us, event | category | flops | bytes accessed | tf_op | source)
XLA Modules:
  0.0 109.2 jit_solution(12234599792139348077)
XLA Ops:
  7.2 0.8 convert_bitcast_fusion
  8.0 0.1 copy.82
  8.1 0.1 convert_element_type.75
  8.1 2.1 %fusion.20 = bf16[4,784,128]{2,1,0:T(8,128)(2,1)} fusion(bf16[4,1,12]{2,1,0:T(2,128)(2,1)S(1)} %convert_element_type.75, bf16[4,768,128]{2,1,0:T(8,128)(2,1)} %bitcast.88), kind=kLoop, calls=%fused_computation.27 | loop fusion | flops 2408448 | bytes 1589344 | tf_op jit(solution)/shard_map/concatenate | solution.py:22
  10.2 4.3 %all-to-all-start = ((bf16[4,784,128]{2,1,0:T(8,128)(2,1)}), bf16[4,784,128]{2,1,0:T(8,128)(2,1)}, u32[]{:S(2)}, u32[]{:S(2)}) async-start(bf16[4,784,128]{2,1,0:T(8,128)(2,1)} %fusion.20), calls=%async_computation | async-start | bytes 1605632 | tf_op jit(solution)/shard_map/all_to_all | solution.py:22
  14.5 0.7 copy.88
  15.2 0.7 copy.89
  15.9 11.4 %all-to-all-done = bf16[4,784,128]{2,1,0:T(8,128)(2,1)} async-done(((bf16[4,784,128]{2,1,0:T(8,128)(2,1)}), bf16[4,784,128]{2,1,0:T(8,128)(2,1)}, u32[]{:S(2)}, u32[]{:S(2)}) %all-to-all-start) | async-done | bytes 802848 | tf_op jit(solution)/shard_map/all_to_all | solution.py:22
  27.2 0.7 slice.18
  28.1 0.1 copy.105
  28.2 0.1 copy.104
  28.4 0.7 gather_fusion
  29.1 0.4 copy.90
  29.5 1.2 %slice.21 = bf16[4,768,128]{2,1,0:T(8,128)(2,1)S(1)} slice(bf16[4,784,128]{2,1,0:T(8,128)(2,1)} %all-to-all-done), slice={[0:4], [0:768], [0:128]} | slice | bytes 1572864 | tf_op jit(solution)/shard_map/slice | solution.py:23
  30.7 0.5 multiply_convert_fusion
  31.3 1.1 fusion.17
  32.4 0.1 copy-done
  32.5 3.2 %fusion.19 = (bf16[16,8,32,128]{3,1,2,0:T(8,128)(2,1)S(1)}, bf16[128,4096]{1,0:T(8,128)(2,1)}) fusion(f32[16,8,32,128]{3,2,1,0:T(8,128)S(1)} %bitcast.78, bf16[128,4096]{1,0:T(8,128)(2,1)S(1)} %copy-done), kind=kLoop, calls=%fused_computation.26 | loop fusion | flops 12058624 | bytes 5242880
  35.7 0.2 copy.108
  36.0 0.4 fusion.30
  36.4 0.7 fusion.26
  37.1 4.0 %fusion.13 = f32[32,128,128]{2,0,1:T(8,128)} fusion(f32[4,6,128,128]{3,2,1,0:T(8,128)S(1)} %fusion.26, s32[4,6]{1,0:T(4,128)S(1)} %get-tuple-element.9, pred[4,6]{1,0:T(4,128)(4,1)S(1)} %get-tuple-element.4), kind=kOutput, calls=%fused_computation.19 | convolution fusion | flops 150996480 | bytes 3670136 | tf_op jit(solution)/shard_map/mctk,mcr->rtk/dot_general | solution.py:52
  41.1 0.4 fusion.21
  41.5 0.3 copy.95
  41.9 5.0 %all_to_all.20 = f32[2,384,4,128]{3,1,2,0:T(8,128)S(1)} all-to-all(f32[2,384,4,128]{3,1,2,0:T(8,128)S(1)} %bitcast.79), channel_id=1, replica_groups=mesh['y'=8,'z'=12,'c'=2,'mp'=4] {'c'}, dimensions={0} | all-to-all | bytes 3145728 | tf_op jit(solution)/shard_map/all_to_all | solution.py:66
  46.9 0.1 copy.96
  47.1 45.0 %all_to_all.21 = bf16[96,4,4,128]{3,1,2,0:T(4,128)(2,1)S(1)} all-to-all(bf16[96,4,4,128]{3,1,2,0:T(4,128)(2,1)S(1)} %copy.96), channel_id=1, replica_groups=mesh['y'=8,'z'=12,'c'=2,'mp'=4] {'y','z'}, dimensions={0} | all-to-all | bytes 786432 | tf_op jit(solution)/shard_map/all_to_all | solution.py:68
  92.1 0.2 convert_reduce_fusion
  92.3 7.6 %all_to_all.22 = f32[4,4,128]{2,0,1:T(4,128)S(1)} all-to-all(f32[4,4,128]{2,0,1:T(4,128)S(1)} %convert_reduce_fusion), channel_id=1, replica_groups=mesh['y'=8,'z'=12,'c'=2,'mp'=4] {'mp'}, dimensions={1} | all-to-all | bytes 16384 | tf_op jit(solution)/shard_map/all_to_all | solution.py:70
  99.9 1.1 convert_element_type.70
  101.0 0.8 copy.130
  101.8 0.6 copy.132
  (17 shorter events, 0.4 us)
Async XLA Ops:
  7.2 7.3 %copy-start.1 = (bf16[128,4096]{1,0:T(8,128)(2,1)S(1)}, bf16[128,4096]{1,0:T(8,128)(2,1)}, u32[]{:S(2)}) copy-start(bf16[128,4096]{1,0:T(8,128)(2,1)} %param.5) | copy-start | bytes 3145732
  10.2 17.0 %all-to-all-start = ((bf16[4,784,128]{2,1,0:T(8,128)(2,1)}), bf16[4,784,128]{2,1,0:T(8,128)(2,1)}, u32[]{:S(2)}, u32[]{:S(2)}) async-start(bf16[4,784,128]{2,1,0:T(8,128)(2,1)} %fusion.20), calls=%async_computation | async-start | bytes 1605632 | tf_op jit(solution)/shard_map/all_to_all | solution.py:22
  14.5 85.4 %reduce-scatter.2.cloned.1.call-start = ((), (), s32[]{:S(2)}) async-start(), calls=%async_computation.5 | async-start | bytes 2621440 | tf_op jit(solution)/shard_map/reduce_scatter | solution.py:55
  31.3 1.2 %copy-start = (bf16[128,4096]{1,0:T(8,128)(2,1)S(1)}, bf16[128,4096]{1,0:T(8,128)(2,1)}, u32[]{:S(2)}) copy-start(bf16[128,4096]{1,0:T(8,128)(2,1)} %param.9) | copy-start | bytes 3145732
Sparse Core Ops, SparseCore 0:
  41.2 42.5 reduce-scatter.1

commit v7 on v6

--- a/solution.py
+++ b/solution.py
@@ -52,7 +52,12 @@
     input_partial = jnp.einsum(
         "mctk,mcr->rtk", input_terms, row_onehot, precision=lax.Precision.HIGHEST
     )
-    input_grad = lax.psum_scatter(input_partial, "mp", scatter_dimension=0, tiled=True)
+    pieces = input_partial.reshape(mp_count, row_blocks // mp_count, token_count, block_size)
+    input_grad = lax.dynamic_index_in_dim(pieces, column_here, 0, keepdims=False)
+    for shift in range(1, mp_count):
+        piece = lax.dynamic_index_in_dim(pieces, (column_here + shift) % mp_count, 0, keepdims=False)
+        ring = [(k, (k + shift) % mp_count) for k in range(mp_count)]
+        input_grad = input_grad + lax.ppermute(piece, "mp", ring)
     input_grad = jnp.transpose(input_grad.astype(jnp.bfloat16), (1, 0, 2))
     input_grad = input_grad.reshape(token_count, row_blocks * block_size // mp_count)
     weight_terms = jnp.einsum(

time: 110 us -> 98.8 us (0.90)
  the two profiles are of different devices: /device:TPU:8 before, /device:TPU:6 now
where the time goes in v7:
time: 98.8 us; the launch traced here: 98.2 us
  starting transfers between devices  44.9 us (45%)
  waiting for transfers between devices  22.4 us (23%)
  local copies, waits for them, and re-layouts  10.1 us (10%)
  other arithmetic  9.22 us (9%)
  matrix products  5.76 us (6%)
  blocking collectives  5 us (5%)
    all_to_all x1, starting transfers between devices, body(): lax.all_to_all(staged.astype(jnp.bfloat16), ('y', 'z'), 0, 0, tiled=True)  16.2 us
    all_to_all x1, starting transfers between devices, body(): lax.all_to_all(jnp.concatenate([w_groups, lists], 1), 'mp', 0, 0, tiled=T...  13.6 us
    ppermute x3, starting transfers between devices, body(): input_grad = input_grad + lax.ppermute(piece, 'mp', ring)  9.82 us
    all_to_all x1, waiting for transfers between devices, body(): lax.all_to_all(staged.astype(jnp.bfloat16), ('y', 'z'), 0, 0, tiled=True)  8.16 us
    ppermute x3, waiting for transfers between devices, body(): input_grad = input_grad + lax.ppermute(piece, 'mp', ring)  8 us
    all_to_all x1, waiting for transfers between devices, body(): lax.all_to_all(jnp.concatenate([w_groups, lists], 1), 'mp', 0, 0, tiled=T...  6.26 us
    all_to_all x1, starting transfers between devices, body(): staged = lax.all_to_all(staged, 'mp', 1, 1, tiled=True)  5.29 us
    all_to_all x1, blocking collectives, body(): staged = lax.all_to_all(staged, 'c', 0, 0, tiled=True).sum(0)  5 us
  transfers between devices with their start and end apart: 6, of which 4 were waited for; matrix products, arithmetic and copies ran while one was open for 9% of the time, Pallas kernels for 0%

profile of v7, /device:TPU:6, one launch (start us, length us, event | category | flops | bytes accessed | tf_op | source)
XLA Modules:
  0.0 98.2 jit_solution(5456674105968914336)
XLA Ops:
  0.6 0.8 convert_bitcast_fusion
  1.6 2.1 %fusion.20 = bf16[4,784,128]{2,1,0:T(8,128)(2,1)} fusion(bf16[4,1,12]{2,1,0:T(2,128)(2,1)S(1)} %convert_element_type.75, bf16[4,768,128]{2,1,0:T(8,128)(2,1)} %bitcast.104), kind=kLoop, calls=%fused_computation.27 | loop fusion | flops 2408448 | bytes 1589344 | tf_op jit(solution)/shard_map/concatenate | solution.py:22
  3.7 13.6 %all-to-all-start = ((bf16[4,784,128]{2,1,0:T(8,128)(2,1)}), bf16[4,784,128]{2,1,0:T(8,128)(2,1)}, u32[]{:S(2)}, u32[]{:S(2)}) async-start(bf16[4,784,128]{2,1,0:T(8,128)(2,1)} %fusion.20), calls=%async_computation | async-start | bytes 1605632 | tf_op jit(solution)/shard_map/all_to_all | solution.py:22
  17.3 0.7 copy.88
  18.0 0.7 copy.89
  18.7 6.3 %all-to-all-done = bf16[4,784,128]{2,1,0:T(8,128)(2,1)} async-done(((bf16[4,784,128]{2,1,0:T(8,128)(2,1)}), bf16[4,784,128]{2,1,0:T(8,128)(2,1)}, u32[]{:S(2)}, u32[]{:S(2)}) %all-to-all-start) | async-done | bytes 802848 | tf_op jit(solution)/shard_map/all_to_all | solution.py:22
  24.9 0.7 slice.18
  26.1 0.7 gather_fusion
  27.2 1.2 %slice.21 = bf16[4,768,128]{2,1,0:T(8,128)(2,1)S(1)} slice(bf16[4,784,128]{2,1,0:T(8,128)(2,1)} %all-to-all-done), slice={[0:4], [0:768], [0:128]} | slice | bytes 1572864 | tf_op jit(solution)/shard_map/slice | solution.py:23
  28.4 0.5 multiply_convert_fusion
  29.0 1.0 %fusion.17 = f32[32,128,128,1]{2,0,3,1:T(8,128)S(1)} fusion(bf16[4,6,128,128]{3,2,1,0:T(8,128)(2,1)S(1)} %multiply_convert_fusion, s32[4,6]{1,0:T(4,128)S(1)} %subtract_bitcast_fusion), kind=kOutput, calls=%fused_computation.24 | convolution fusion | flops 25166592 | bytes 2883680 | tf_op jit(solution)/shard_map/mctn,mcj->tjn/dot_general | solution.py:37
  30.2 3.2 %fusion.19 = (bf16[16,8,32,128]{3,1,2,0:T(8,128)(2,1)S(1)}, bf16[128,4096]{1,0:T(8,128)(2,1)}) fusion(f32[16,8,32,128]{3,2,1,0:T(8,128)S(1)} %bitcast.94, bf16[128,4096]{1,0:T(8,128)(2,1)S(1)} %copy-done), kind=kLoop, calls=%fused_computation.26 | loop fusion | flops 12058624 | bytes 5242880
  33.7 0.4 fusion.33
  34.1 0.4 fusion.21
  34.8 5.0 %all_to_all.20 = f32[2,384,4,128]{3,1,2,0:T(8,128)S(1)} all-to-all(f32[2,384,4,128]{3,1,2,0:T(8,128)S(1)} %bitcast.95), channel_id=1, replica_groups=mesh['y'=8,'z'=12,'c'=2,'mp'=4] {'c'}, dimensions={0} | all-to-all | bytes 3145728 | tf_op jit(solution)/shard_map/all_to_all | solution.py:71
  39.8 0.9 reduce_sum.18
  40.8 1.9 %copy.96 = bf16[96,4,4,128]{3,1,2,0:T(4,128)(2,1)} copy(bf16[96,4,4,128]{3,1,0,2:T(4,128)(2,1)} %bitcast.102) | data formatting | bytes 786432 | tf_op jit(solution)/shard_map/convert_element_type | solution.py:73
  42.7 16.2 %all-to-all-start.2 = ((bf16[96,4,4,128]{3,1,2,0:T(4,128)(2,1)}), bf16[96,4,4,128]{3,1,2,0:T(4,128)(2,1)S(1)}, u32[]{:S(2)}, u32[]{:S(2)}) async-start(bf16[96,4,4,128]{3,1,2,0:T(4,128)(2,1)} %copy.96), calls=%async_computation.2 | async-start | bytes 786432 | tf_op jit(solution)/shard_map/all_to_all | solution.py:73
  58.8 0.7 fusion.29
  59.5 2.7 %fusion.13 = f32[4,8,128,128]{3,1,0,2:T(8,128)S(1)} fusion(f32[4,6,128,128]{3,2,1,0:T(8,128)S(1)} %fusion.29, s32[4,6]{1,0:T(4,128)S(1)} %get-tuple-element.12, pred[4,6]{1,0:T(4,128)(4,1)S(1)} %get-tuple-element.4), kind=kOutput, calls=%fused_computation.19 | convolution fusion | flops 150996480 | bytes 3670136 | tf_op jit(solution)/shard_map/mctk,mcr->rtk/dot_general | solution.py:52
  62.2 1.2 %dynamic-slice_bitcast_fusion.2 = (f32[8,128,128]{2,0,1:T(8,128)}, f32[8,128,128]{2,0,1:T(8,128)}, f32[8,128,128]{2,0,1:T(8,128)S(1)}) fusion(f32[4,8,128,128]{3,1,0,2:T(8,128)S(1)} %fusion.13, s32[]{:T(128)S(6)} %select_n.38, s32[]{:T(128)S(6)} %select_n.42, s32[]{:T(128)S(6)} %select_n.40), kind=kLoop, calls=%fused_computation.39 | loop fusion | bytes 3145740 | tf_op jit(solution)/shard_map/jit(dynamic_index_in_dim)/squeeze | solution.py:58
  63.4 4.0 %collective-permute-start = (f32[8,128,128]{2,0,1:T(8,128)}, f32[8,128,128]{2,0,1:T(8,128)S(1)}, u32[]{:S(2)}, u32[]{:S(2)}) collective-permute-start(f32[8,128,128]{2,0,1:T(8,128)} %get-tuple-element.5), channel_id=1, source_target_pairs={{0,1},{1,2},{2,3},{3,0},{4,5},{5,6},{6,7},{7,4},{8,9},{9,10},{10,1... | collective-permute-start | bytes 1572872 | tf_op jit(solution)/shard_map/ppermute | solution.py:60
  67.4 1.9 %collective-permute-start.2 = (f32[8,128,128]{2,0,1:T(8,128)}, f32[8,128,128]{2,0,1:T(8,128)}, u32[]{:S(2)}, u32[]{:S(2)}) collective-permute-start(f32[8,128,128]{2,0,1:T(8,128)} %get-tuple-element.6), channel_id=1, source_target_pairs={{0,3},{1,0},{2,1},{3,2},{4,7},{5,4},{6,5},{7,6},{8,11},{9,8},{10,9... | collective-permute-start | bytes 1572872 | tf_op jit(solution)/shard_map/ppermute | solution.py:60
  69.3 3.9 %collective-permute-start.1 = (f32[8,128,128]{2,0,1:T(8,128)S(1)}, f32[8,128,128]{2,0,1:T(8,128)}, u32[]{:S(2)}, u32[]{:S(2)}) collective-permute-start(f32[8,128,128]{2,0,1:T(8,128)S(1)} %get-tuple-element.7), channel_id=1, source_target_pairs={{0,2},{1,3},{2,0},{3,1},{4,6},{5,7},{6,4},{7,5},{8,10},{9,11},{10,... | collective-permute-start | bytes 1572872 | tf_op jit(solution)/shard_map/ppermute | solution.py:60
  73.2 8.2 %all-to-all-done.2 = bf16[96,4,4,128]{3,1,2,0:T(4,128)(2,1)S(1)} async-done(((bf16[96,4,4,128]{3,1,2,0:T(4,128)(2,1)}), bf16[96,4,4,128]{3,1,2,0:T(4,128)(2,1)S(1)}, u32[]{:S(2)}, u32[]{:S(2)}) %all-to-all-start.2) | async-done | bytes 393248 | tf_op jit(solution)/shard_map/all_to_all | solution.py:73
  81.4 0.8 convert_reduce_fusion
  82.2 5.3 %all-to-all-start.3 = ((f32[4,4,128]{2,0,1:T(4,128)}), f32[4,4,128]{2,0,1:T(4,128)S(1)}, u32[]{:S(2)}, u32[]{:S(2)}) async-start(f32[4,4,128]{2,0,1:T(4,128)} %convert_reduce_fusion), calls=%async_computation.3 | async-start | bytes 16384 | tf_op jit(solution)/shard_map/all_to_all | solution.py:75
  87.5 2.7 %collective-permute-done = f32[8,128,128]{2,0,1:T(8,128)S(1)} collective-permute-done((f32[8,128,128]{2,0,1:T(8,128)}, f32[8,128,128]{2,0,1:T(8,128)S(1)}, u32[]{:S(2)}, u32[]{:S(2)}) %collective-permute-start) | collective-permute-done | bytes 524320 | tf_op jit(solution)/shard_map/ppermute | solution.py:60
  90.2 5.3 %collective-permute-done.2 = f32[8,128,128]{2,0,1:T(8,128)} collective-permute-done((f32[8,128,128]{2,0,1:T(8,128)}, f32[8,128,128]{2,0,1:T(8,128)}, u32[]{:S(2)}, u32[]{:S(2)}) %collective-permute-start.2) | collective-permute-done | bytes 524320 | tf_op jit(solution)/shard_map/ppermute | solution.py:60
  95.5 1.3 %fusion.26 = bf16[8,128,128]{2,0,1:T(8,128)(2,1)S(1)} fusion(f32[8,128,128]{2,0,1:T(8,128)} %collective-permute-done.2, f32[8,128,128]{2,0,1:T(8,128)} %collective-permute-done.1, f32[8,128,128]{2,0,1:T(8,128)S(1)} %collective-permute-done, f32[4,8,128,128]{3,1,0,2:T(8,128)S(1)} %fusion.13, s32[]{:T(128)S(6)} %select_n.36), kind=kLoop, calls=%fused_computation.36 | loop fusion | flops 524288 | bytes 2359300 | tf_op jit(solution)/shard_map/convert_element_type | solution.py:61
  96.8 0.8 copy.130
  97.6 0.6 copy.132
  (23 shorter events, 1.8 us)
Async XLA Ops:
  0.6 16.7 %copy-start.1 = (bf16[128,4096]{1,0:T(8,128)(2,1)S(1)}, bf16[128,4096]{1,0:T(8,128)(2,1)}, u32[]{:S(2)}) copy-start(bf16[128,4096]{1,0:T(8,128)(2,1)} %param.5) | copy-start | bytes 3145732
  3.7 21.2 %all-to-all-start = ((bf16[4,784,128]{2,1,0:T(8,128)(2,1)}), bf16[4,784,128]{2,1,0:T(8,128)(2,1)}, u32[]{:S(2)}, u32[]{:S(2)}) async-start(bf16[4,784,128]{2,1,0:T(8,128)(2,1)} %fusion.20), calls=%async_computation | async-start | bytes 1605632 | tf_op jit(solution)/shard_map/all_to_all | solution.py:22
  28.9 1.2 %copy-start = (bf16[128,4096]{1,0:T(8,128)(2,1)S(1)}, bf16[128,4096]{1,0:T(8,128)(2,1)}, u32[]{:S(2)}) copy-start(bf16[128,4096]{1,0:T(8,128)(2,1)} %param.9) | copy-start | bytes 3145732
  42.7 38.7 %all-to-all-start.2 = ((bf16[96,4,4,128]{3,1,2,0:T(4,128)(2,1)}), bf16[96,4,4,128]{3,1,2,0:T(4,128)(2,1)S(1)}, u32[]{:S(2)}, u32[]{:S(2)}) async-start(bf16[96,4,4,128]{3,1,2,0:T(4,128)(2,1)} %copy.96), calls=%async_computation.2 | async-start | bytes 786432 | tf_op jit(solution)/shard_map/all_to_all | solution.py:73
  63.4 26.8 %collective-permute-start = (f32[8,128,128]{2,0,1:T(8,128)}, f32[8,128,128]{2,0,1:T(8,128)S(1)}, u32[]{:S(2)}, u32[]{:S(2)}) collective-permute-start(f32[8,128,128]{2,0,1:T(8,128)} %get-tuple-element.5), channel_id=1, source_target_pairs={{0,1},{1,2},{2,3},{3,0},{4,5},{5,6},{6,7},{7,4},{8,9},{9,10},{10,1... | collective-permute-start | bytes 1572872 | tf_op jit(solution)/shard_map/ppermute | solution.py:60
  67.4 28.1 %collective-permute-start.2 = (f32[8,128,128]{2,0,1:T(8,128)}, f32[8,128,128]{2,0,1:T(8,128)}, u32[]{:S(2)}, u32[]{:S(2)}) collective-permute-start(f32[8,128,128]{2,0,1:T(8,128)} %get-tuple-element.6), channel_id=1, source_target_pairs={{0,3},{1,0},{2,1},{3,2},{4,7},{5,4},{6,5},{7,6},{8,11},{9,8},{10,9... | collective-permute-start | bytes 1572872 | tf_op jit(solution)/shard_map/ppermute | solution.py:60
  69.3 26.2 %collective-permute-start.1 = (f32[8,128,128]{2,0,1:T(8,128)S(1)}, f32[8,128,128]{2,0,1:T(8,128)}, u32[]{:S(2)}, u32[]{:S(2)}) collective-permute-start(f32[8,128,128]{2,0,1:T(8,128)S(1)} %get-tuple-element.7), channel_id=1, source_target_pairs={{0,2},{1,3},{2,0},{3,1},{4,6},{5,7},{6,4},{7,5},{8,10},{9,11},{10,... | collective-permute-start | bytes 1572872 | tf_op jit(solution)/shard_map/ppermute | solution.py:60
  82.2 15.4 %all-to-all-start.3 = ((f32[4,4,128]{2,0,1:T(4,128)}), f32[4,4,128]{2,0,1:T(4,128)S(1)}, u32[]{:S(2)}, u32[]{:S(2)}) async-start(f32[4,4,128]{2,0,1:T(4,128)} %convert_reduce_fusion), calls=%async_computation.3 | async-start | bytes 16384 | tf_op jit(solution)/shard_map/all_to_all | solution.py:75

commit v8 on v6

--- a/solution.py
+++ b/solution.py
@@ -46,19 +46,25 @@
     input_terms = jnp.einsum(
         "mctn,mckn->mctk", grad_cols, w_here, preferred_element_type=jnp.float32
     )
+    local_row = (row_groups - column_here * (row_blocks // mp_count)) % row_blocks
     row_onehot = (
-        (row_groups[:, :, None] == jnp.arange(row_blocks)[None, None, :]) & slot_live[:, :, None]
+        (local_row[:, :, None] == jnp.arange(row_blocks)[None, None, :]) & slot_live[:, :, None]
     ).astype(jnp.float32)
     input_partial = jnp.einsum(
         "mctk,mcr->rtk", input_terms, row_onehot, precision=lax.Precision.HIGHEST
     )
-    input_grad = lax.psum_scatter(input_partial, "mp", scatter_dimension=0, tiled=True)
-    input_grad = jnp.transpose(input_grad.astype(jnp.bfloat16), (1, 0, 2))
-    input_grad = input_grad.reshape(token_count, row_blocks * block_size // mp_count)
+    pieces = input_partial.reshape(mp_count, row_blocks // mp_count, token_count, block_size)
     weight_terms = jnp.einsum(
         "tmck,mctn->mckn", picked_x, grad_cols, preferred_element_type=jnp.float32
     )
     weight_terms = weight_terms.reshape(mp_count, slot_cap * block_size, block_size)
+    weight_terms, pieces = lax.optimization_barrier((weight_terms, pieces))
+    input_grad = pieces[0]
+    for shift in range(1, mp_count):
+        ring = [(k, (k + shift) % mp_count) for k in range(mp_count)]
+        input_grad = input_grad + lax.ppermute(pieces[shift], "mp", ring)
+    input_grad = jnp.transpose(input_grad.astype(jnp.bfloat16), (1, 0, 2))
+    input_grad = input_grad.reshape(token_count, row_blocks * block_size // mp_count)
     ny, nz, nc = lax.axis_size("y"), lax.axis_size("z"), lax.axis_size("c")
     rows = slot_cap * block_size // (ny * nz * nc)
     staged = weight_terms.reshape(mp_count, ny, nz, nc, rows, block_size)

time: 110 us -> 99.4 us (0.904)
  blocking collectives: 57.7 us -> 5.84 us
  starting transfers between devices: 4.29 us -> 37.7 us
  waiting for transfers between devices: 11.4 us -> 29.8 us
  between operations: 14.1 us -> 0.81 us
  other arithmetic: 7.48 us -> 9.8 us
  local copies, waits for them, and re-layouts: 7.11 us -> 8.96 us
  matrix products: 7.14 us -> 5.81 us
    all_to_all x2 -> x0, blocking collectives: 52.7 us -> none  [the longest x1 45 us: body(): lax.all_to_all(staged.astype(jnp.bfloat16), ('y', 'z'), 0, 0, tiled=True)]
    all_to_all x0 -> x2, starting transfers between devices: none -> 25 us  [the longest x1 21.8 us: body(): lax.all_to_all(staged.astype(jnp.bfloat16), ('y', 'z'), 0, 0, tiled=True)]
    all_to_all x0 -> x2, waiting for transfers between devices: none -> 13.9 us  [the longest x1 13.9 us: body(): lax.all_to_all(staged.astype(jnp.bfloat16), ('y', 'z'), 0, 0, tiled=True)]
    ppermute x0 -> x3, starting transfers between devices: none -> 8.36 us  [body(): input_grad = input_grad + lax.ppermute(pieces[shift], 'mp', ring)]
    ppermute x0 -> x3, waiting for transfers between devices: none -> 4.52 us  [body(): input_grad = input_grad + lax.ppermute(pieces[shift], 'mp', ring)]
    reduce_sum x1, other arithmetic: 0.07 us -> 1.54 us  [body(): staged = lax.all_to_all(staged, 'c', 0, 0, tiled=True).sum(0)]
    dot_general x1, matrix products: 4.03 us -> 2.69 us  [body(): jnp.einsum('mctk,mcr->rtk', input_terms, row_onehot, precision=lax.Precis...]
    squeeze x0 -> x2, local copies, waits for them, and re-layouts: none -> 1.11 us  [body(): input_grad = input_grad + lax.ppermute(pieces[shift], 'mp', ring)]
  transfers between devices with their start and end apart: 2 -> 6, of which waited for: 1 -> 3; matrix products, arithmetic and copies ran while one was open for 2% -> 5% of each run, Pallas kernels for 0% -> 0%
where the time goes in v8:
time: 99.4 us; the launch traced here: 98.7 us
  starting transfers between devices  37.7 us (38%)
  waiting for transfers between devices  29.8 us (30%)
  other arithmetic  9.8 us (10%)
  local copies, waits for them, and re-layouts  8.96 us (9%)
  blocking collectives  5.84 us (6%)
  matrix products  5.81 us (6%)
    all_to_all x1, starting transfers between devices, body(): lax.all_to_all(staged.astype(jnp.bfloat16), ('y', 'z'), 0, 0, tiled=True)  21.8 us
    all_to_all x1, waiting for transfers between devices, body(): lax.all_to_all(staged.astype(jnp.bfloat16), ('y', 'z'), 0, 0, tiled=True)  13.9 us
    all_to_all x1, waiting for transfers between devices, body(): lax.all_to_all(jnp.concatenate([w_groups, lists], 1), 'mp', 0, 0, tiled=T...  11.4 us
    ppermute x3, starting transfers between devices, body(): input_grad = input_grad + lax.ppermute(pieces[shift], 'mp', ring)  8.36 us
    all_to_all x1, blocking collectives, body(): staged = lax.all_to_all(staged, 'c', 0, 0, tiled=True).sum(0)  5.84 us
    ppermute x3, waiting for transfers between devices, body(): input_grad = input_grad + lax.ppermute(pieces[shift], 'mp', ring)  4.52 us
    all_to_all x1, starting transfers between devices, body(): lax.all_to_all(jnp.concatenate([w_groups, lists], 1), 'mp', 0, 0, tiled=T...  4.29 us
    all_to_all x1, starting transfers between devices, body(): staged = lax.all_to_all(staged, 'mp', 1, 1, tiled=True)  3.25 us
  transfers between devices with their start and end apart: 6, of which 3 were waited for; matrix products, arithmetic and copies ran while one was open for 5% of the time, Pallas kernels for 0%

profile of v8, /device:TPU:8, one launch (start us, length us, event | category | flops | bytes accessed | tf_op | source)
XLA Modules:
  0.0 98.7 jit_solution(16556164156774225822)
XLA Ops:
  0.6 0.8 convert_bitcast_fusion
  1.6 2.1 %fusion.20 = bf16[4,784,128]{2,1,0:T(8,128)(2,1)} fusion(bf16[4,1,12]{2,1,0:T(2,128)(2,1)S(1)} %convert_element_type.75, bf16[4,768,128]{2,1,0:T(8,128)(2,1)} %bitcast.107), kind=kLoop, calls=%fused_computation.27 | loop fusion | flops 2408448 | bytes 1589344 | tf_op jit(solution)/shard_map/concatenate | solution.py:22
  3.7 4.3 %all-to-all-start = ((bf16[4,784,128]{2,1,0:T(8,128)(2,1)}), bf16[4,784,128]{2,1,0:T(8,128)(2,1)}, u32[]{:S(2)}, u32[]{:S(2)}) async-start(bf16[4,784,128]{2,1,0:T(8,128)(2,1)} %fusion.20), calls=%async_computation | async-start | bytes 1605632 | tf_op jit(solution)/shard_map/all_to_all | solution.py:22
  8.0 0.7 copy.102
  8.6 0.7 copy.103
  9.3 11.4 %all-to-all-done = bf16[4,784,128]{2,1,0:T(8,128)(2,1)} async-done(((bf16[4,784,128]{2,1,0:T(8,128)(2,1)}), bf16[4,784,128]{2,1,0:T(8,128)(2,1)}, u32[]{:S(2)}, u32[]{:S(2)}) %all-to-all-start) | async-done | bytes 802848 | tf_op jit(solution)/shard_map/all_to_all | solution.py:22
  20.7 0.7 slice.34
  21.9 0.7 gather_fusion
  22.6 0.4 copy.104
  23.0 1.2 %slice.37 = bf16[4,768,128]{2,1,0:T(8,128)(2,1)S(1)} slice(bf16[4,784,128]{2,1,0:T(8,128)(2,1)} %all-to-all-done), slice={[0:4], [0:768], [0:128]} | slice | bytes 1572864 | tf_op jit(solution)/shard_map/slice | solution.py:23
  24.2 0.5 multiply_convert_fusion
  24.7 1.1 %fusion.17 = f32[32,128,128,1]{2,0,3,1:T(8,128)S(1)} fusion(bf16[4,6,128,128]{3,2,1,0:T(8,128)(2,1)S(1)} %multiply_convert_fusion, s32[4,6]{1,0:T(4,128)S(1)} %subtract_bitcast_fusion), kind=kOutput, calls=%fused_computation.24 | convolution fusion | flops 25166592 | bytes 2883680 | tf_op jit(solution)/shard_map/mctn,mcj->tjn/dot_general | solution.py:37
  25.9 3.2 %fusion.19 = (bf16[16,8,32,128]{3,1,2,0:T(8,128)(2,1)S(1)}, bf16[128,4096]{1,0:T(8,128)(2,1)}) fusion(f32[16,8,32,128]{3,2,1,0:T(8,128)S(1)} %bitcast.97, bf16[128,4096]{1,0:T(8,128)(2,1)S(1)} %copy-done), kind=kLoop, calls=%fused_computation.26 | loop fusion | flops 12058624 | bytes 5242880
  29.4 0.4 fusion.34
  29.9 0.4 fusion.21
  30.3 0.7 fusion.30
  31.0 2.7 %fusion.13 = f32[4,8,128,128]{3,1,0,2:T(8,128)S(1)} fusion(f32[4,6,128,128]{3,2,1,0:T(8,128)S(1)} %fusion.30, s32[4,6]{1,0:T(4,128)S(1)} %get-tuple-element.15, pred[4,6]{1,0:T(4,128)(4,1)S(1)} %get-tuple-element.8), kind=kOutput, calls=%fused_computation.19 | convolution fusion | flops 150996480 | bytes 3670136 | tf_op jit(solution)/shard_map/mctk,mcr->rtk/dot_general | solution.py:53
  34.0 5.8 %all_to_all.20 = f32[2,384,4,128]{3,1,2,0:T(8,128)} all-to-all(f32[2,384,4,128]{3,1,2,0:T(8,128)S(1)} %bitcast.98), channel_id=1, replica_groups=mesh['y'=8,'z'=12,'c'=2,'mp'=4] {'c'}, dimensions={0} | all-to-all | bytes 3145728 | tf_op jit(solution)/shard_map/all_to_all | solution.py:72
  39.8 1.5 %reduce_sum.18 = bf16[384,4,128]{2,0,1:T(8,128)(2,1)S(1)} reduce(f32[2,384,4,128]{3,1,2,0:T(8,128)} %all_to_all.20, f32[]{:T(128)} %constant.53.clone.1), dimensions={0}, to_apply=%region_0.1 | reduce | flops 196608 | bytes 1966084 | tf_op jit(solution)/shard_map/reduce_sum | solution.py:72
  41.4 0.9 copy.113
  42.2 21.8 %all-to-all-start.2 = ((bf16[96,4,4,128]{3,1,2,0:T(4,128)(2,1)}), bf16[96,4,4,128]{3,1,2,0:T(4,128)(2,1)S(1)}, u32[]{:S(2)}, u32[]{:S(2)}) async-start(bf16[96,4,4,128]{3,1,2,0:T(4,128)(2,1)} %copy.113), calls=%async_computation.2 | async-start | bytes 786432 | tf_op jit(solution)/shard_map/all_to_all | solution.py:74
  64.1 3.1 %collective-permute-start.2 = (f32[8,128,128]{2,0,1:T(8,128)S(1)}, f32[8,128,128]{2,0,1:T(8,128)S(1)}, u32[]{:S(2)}, u32[]{:S(2)}) collective-permute-start(f32[8,128,128]{2,0,1:T(8,128)S(1)} %slice_bitcast_fusion.3), channel_id=1, source_target_pairs={{0,3},{1,0},{2,1},{3,2},{4,7},{5,4},{6,5},{7,6},{8,11},{9,8},{10,9... | collective-permute-start | bytes 1572872 | tf_op jit(solution)/shard_map/ppermute | solution.py:65
  67.2 1.0 %slice_bitcast_fusion.1 = (f32[8,128,128]{2,0,1:T(8,128)}, f32[8,128,128]{2,0,1:T(8,128)}) fusion(f32[4,8,128,128]{3,1,0,2:T(8,128)S(1)} %fusion.13), kind=kLoop, calls=%fused_computation.34 | loop fusion | bytes 2097152 | tf_op jit(solution)/shard_map/squeeze | solution.py:65
  68.2 2.8 %collective-permute-start = (f32[8,128,128]{2,0,1:T(8,128)}, f32[8,128,128]{2,0,1:T(8,128)}, u32[]{:S(2)}, u32[]{:S(2)}) collective-permute-start(f32[8,128,128]{2,0,1:T(8,128)} %get-tuple-element.9), channel_id=1, source_target_pairs={{0,1},{1,2},{2,3},{3,0},{4,5},{5,6},{6,7},{7,4},{8,9},{9,10},{10,1... | collective-permute-start | bytes 1572872 | tf_op jit(solution)/shard_map/ppermute | solution.py:65
  71.0 2.5 %collective-permute-start.1 = (f32[8,128,128]{2,0,1:T(8,128)}, f32[8,128,128]{2,0,1:T(8,128)}, u32[]{:S(2)}, u32[]{:S(2)}) collective-permute-start(f32[8,128,128]{2,0,1:T(8,128)} %get-tuple-element.10), channel_id=1, source_target_pairs={{0,2},{1,3},{2,0},{3,1},{4,6},{5,7},{6,4},{7,5},{8,10},{9,11},{10,... | collective-permute-start | bytes 1572872 | tf_op jit(solution)/shard_map/ppermute | solution.py:65
  73.5 13.9 %all-to-all-done.2 = bf16[96,4,4,128]{3,1,2,0:T(4,128)(2,1)S(1)} async-done(((bf16[96,4,4,128]{3,1,2,0:T(4,128)(2,1)}), bf16[96,4,4,128]{3,1,2,0:T(4,128)(2,1)S(1)}, u32[]{:S(2)}, u32[]{:S(2)}) %all-to-all-start.2) | async-done | bytes 393248 | tf_op jit(solution)/shard_map/all_to_all | solution.py:74
  87.5 0.8 convert_reduce_fusion
  88.3 3.2 %all-to-all-start.3 = ((f32[4,4,128]{2,0,1:T(4,128)}), f32[4,4,128]{2,0,1:T(4,128)S(1)}, u32[]{:S(2)}, u32[]{:S(2)}) async-start(f32[4,4,128]{2,0,1:T(4,128)} %convert_reduce_fusion), calls=%async_computation.3 | async-start | bytes 16384 | tf_op jit(solution)/shard_map/all_to_all | solution.py:76
  91.5 4.5 %collective-permute-done = f32[8,128,128]{2,0,1:T(8,128)} collective-permute-done((f32[8,128,128]{2,0,1:T(8,128)}, f32[8,128,128]{2,0,1:T(8,128)}, u32[]{:S(2)}, u32[]{:S(2)}) %collective-permute-start) | collective-permute-done | bytes 524320 | tf_op jit(solution)/shard_map/ppermute | solution.py:65
  96.0 1.3 %fusion.27 = bf16[8,128,128]{2,0,1:T(8,128)(2,1)S(1)} fusion(f32[8,128,128]{2,0,1:T(8,128)S(1)} %collective-permute-done.2, f32[8,128,128]{2,0,1:T(8,128)} %collective-permute-done.1, f32[8,128,128]{2,0,1:T(8,128)} %collective-permute-done, f32[4,8,128,128]{3,1,0,2:T(8,128)S(1)} %fusion.13), kind=kLoop, calls=%fused_computation.39 | loop fusion | flops 524288 | bytes 2359296 | tf_op jit(solution)/shard_map/convert_element_type | solution.py:66
  97.4 0.8 copy.151
  98.1 0.6 copy.153
  (24 shorter events, 1.5 us)
Async XLA Ops:
  0.6 7.3 %copy-start.1 = (bf16[128,4096]{1,0:T(8,128)(2,1)S(1)}, bf16[128,4096]{1,0:T(8,128)(2,1)}, u32[]{:S(2)}) copy-start(bf16[128,4096]{1,0:T(8,128)(2,1)} %param.5) | copy-start | bytes 3145732
  3.7 17.0 %all-to-all-start = ((bf16[4,784,128]{2,1,0:T(8,128)(2,1)}), bf16[4,784,128]{2,1,0:T(8,128)(2,1)}, u32[]{:S(2)}, u32[]{:S(2)}) async-start(bf16[4,784,128]{2,1,0:T(8,128)(2,1)} %fusion.20), calls=%async_computation | async-start | bytes 1605632 | tf_op jit(solution)/shard_map/all_to_all | solution.py:22
  24.7 1.2 %copy-start = (bf16[128,4096]{1,0:T(8,128)(2,1)S(1)}, bf16[128,4096]{1,0:T(8,128)(2,1)}, u32[]{:S(2)}) copy-start(bf16[128,4096]{1,0:T(8,128)(2,1)} %param.9) | copy-start | bytes 3145732
  42.2 45.2 %all-to-all-start.2 = ((bf16[96,4,4,128]{3,1,2,0:T(4,128)(2,1)}), bf16[96,4,4,128]{3,1,2,0:T(4,128)(2,1)S(1)}, u32[]{:S(2)}, u32[]{:S(2)}) async-start(bf16[96,4,4,128]{3,1,2,0:T(4,128)(2,1)} %copy.113), calls=%async_computation.2 | async-start | bytes 786432 | tf_op jit(solution)/shard_map/all_to_all | solution.py:74
  64.1 27.4 %collective-permute-start.2 = (f32[8,128,128]{2,0,1:T(8,128)S(1)}, f32[8,128,128]{2,0,1:T(8,128)S(1)}, u32[]{:S(2)}, u32[]{:S(2)}) collective-permute-start(f32[8,128,128]{2,0,1:T(8,128)S(1)} %slice_bitcast_fusion.3), channel_id=1, source_target_pairs={{0,3},{1,0},{2,1},{3,2},{4,7},{5,4},{6,5},{7,6},{8,11},{9,8},{10,9... | collective-permute-start | bytes 1572872 | tf_op jit(solution)/shard_map/ppermute | solution.py:65
  68.2 27.8 %collective-permute-start = (f32[8,128,128]{2,0,1:T(8,128)}, f32[8,128,128]{2,0,1:T(8,128)}, u32[]{:S(2)}, u32[]{:S(2)}) collective-permute-start(f32[8,128,128]{2,0,1:T(8,128)} %get-tuple-element.9), channel_id=1, source_target_pairs={{0,1},{1,2},{2,3},{3,0},{4,5},{5,6},{6,7},{7,4},{8,9},{9,10},{10,1... | collective-permute-start | bytes 1572872 | tf_op jit(solution)/shard_map/ppermute | solution.py:65
  71.0 25.1 %collective-permute-start.1 = (f32[8,128,128]{2,0,1:T(8,128)}, f32[8,128,128]{2,0,1:T(8,128)}, u32[]{:S(2)}, u32[]{:S(2)}) collective-permute-start(f32[8,128,128]{2,0,1:T(8,128)} %get-tuple-element.10), channel_id=1, source_target_pairs={{0,2},{1,3},{2,0},{3,1},{4,6},{5,7},{6,4},{7,5},{8,10},{9,11},{10,... | collective-permute-start | bytes 1572872 | tf_op jit(solution)/shard_map/ppermute | solution.py:65
  88.3 9.9 %all-to-all-start.3 = ((f32[4,4,128]{2,0,1:T(4,128)}), f32[4,4,128]{2,0,1:T(4,128)S(1)}, u32[]{:S(2)}, u32[]{:S(2)}) async-start(f32[4,4,128]{2,0,1:T(4,128)} %convert_reduce_fusion), calls=%async_computation.3 | async-start | bytes 16384 | tf_op jit(solution)/shard_map/all_to_all | solution.py:76

commit v9 on v7

--- a/solution.py
+++ b/solution.py
@@ -69,9 +69,10 @@
     staged = weight_terms.reshape(mp_count, ny, nz, nc, rows, block_size)
     staged = jnp.transpose(staged, (3, 1, 2, 4, 0, 5)).reshape(nc, -1, mp_count, block_size)
     staged = lax.all_to_all(staged, "c", 0, 0, tiled=True).sum(0)
-    staged = staged.reshape(ny * nz, rows, mp_count, block_size)
-    staged = lax.all_to_all(staged.astype(jnp.bfloat16), ("y", "z"), 0, 0, tiled=True)
-    staged = staged.astype(jnp.float32).sum(0)
+    staged = staged.reshape(ny, nz * rows, mp_count, block_size)
+    staged = lax.all_to_all(staged.astype(jnp.bfloat16), "y", 0, 0, tiled=True)
+    staged = staged.astype(jnp.float32).sum(0).reshape(nz, rows, mp_count, block_size)
+    staged = lax.all_to_all(staged, "z", 0, 0, tiled=True).sum(0)
     staged = lax.all_to_all(staged, "mp", 1, 1, tiled=True)
     summed = jnp.transpose(staged, (1, 0, 2))
     return (activation, input_grad, summed)

time: 98.8 us -> 98.6 us (level)
  the two profiles are of different devices: /device:TPU:6 before, /device:TPU:8 now
where the time goes in v9:
time: 98.6 us; the launch traced here: 97.9 us
  starting transfers between devices  40.1 us (41%)
  waiting for transfers between devices  26.5 us (27%)
  local copies, waits for them, and re-layouts  10.6 us (11%)
  other arithmetic  9.09 us (9%)
  matrix products  5.75 us (6%)
  blocking collectives  5 us (5%)
    all_to_all x1, starting transfers between devices, body(): staged = lax.all_to_all(staged, 'z', 0, 0, tiled=True).sum(0)  12.8 us
    all_to_all x1, waiting for transfers between devices, body(): staged = lax.all_to_all(staged, 'z', 0, 0, tiled=True).sum(0)  11.6 us
    all_to_all x1, waiting for transfers between devices, body(): lax.all_to_all(jnp.concatenate([w_groups, lists], 1), 'mp', 0, 0, tiled=T...  11.4 us
    all_to_all x1, starting transfers between devices, body(): staged = lax.all_to_all(staged.astype(jnp.bfloat16), 'y', 0, 0, tiled=True)  9.63 us
    ppermute x3, starting transfers between devices, body(): input_grad = input_grad + lax.ppermute(piece, 'mp', ring)  8.96 us
    all_to_all x1, blocking collectives, body(): staged = lax.all_to_all(staged, 'c', 0, 0, tiled=True).sum(0)  5 us
    all_to_all x1, starting transfers between devices, body(): staged = lax.all_to_all(staged, 'mp', 1, 1, tiled=True)  4.41 us
    all_to_all x1, starting transfers between devices, body(): lax.all_to_all(jnp.concatenate([w_groups, lists], 1), 'mp', 0, 0, tiled=T...  4.29 us
  transfers between devices with their start and end apart: 7, of which 4 were waited for; matrix products, arithmetic and copies ran while one was open for 9% of the time, Pallas kernels for 0%

profile of v9, /device:TPU:8, one launch (start us, length us, event | category | flops | bytes accessed | tf_op | source)
XLA Modules:
  0.0 97.9 jit_solution(15498212822369538754)
XLA Ops:
  0.6 0.8 convert_bitcast_fusion
  1.6 2.1 %fusion.20 = bf16[4,784,128]{2,1,0:T(8,128)(2,1)} fusion(bf16[4,1,12]{2,1,0:T(2,128)(2,1)S(1)} %convert_element_type.75, bf16[4,768,128]{2,1,0:T(8,128)(2,1)} %bitcast.105), kind=kLoop, calls=%fused_computation.27 | loop fusion | flops 2408448 | bytes 1589344 | tf_op jit(solution)/shard_map/concatenate | solution.py:22
  3.7 4.3 %all-to-all-start = ((bf16[4,784,128]{2,1,0:T(8,128)(2,1)}), bf16[4,784,128]{2,1,0:T(8,128)(2,1)}, u32[]{:S(2)}, u32[]{:S(2)}) async-start(bf16[4,784,128]{2,1,0:T(8,128)(2,1)} %fusion.20), calls=%async_computation | async-start | bytes 1605632 | tf_op jit(solution)/shard_map/all_to_all | solution.py:22
  8.0 0.7 copy.109
  8.6 0.7 copy.110
  9.3 11.4 %all-to-all-done = bf16[4,784,128]{2,1,0:T(8,128)(2,1)} async-done(((bf16[4,784,128]{2,1,0:T(8,128)(2,1)}), bf16[4,784,128]{2,1,0:T(8,128)(2,1)}, u32[]{:S(2)}, u32[]{:S(2)}) %all-to-all-start) | async-done | bytes 802848 | tf_op jit(solution)/shard_map/all_to_all | solution.py:22
  20.7 0.7 slice.18
  21.9 0.7 gather_fusion
  23.0 1.2 %slice.21 = bf16[4,768,128]{2,1,0:T(8,128)(2,1)S(1)} slice(bf16[4,784,128]{2,1,0:T(8,128)(2,1)} %all-to-all-done), slice={[0:4], [0:768], [0:128]} | slice | bytes 1572864 | tf_op jit(solution)/shard_map/slice | solution.py:23
  24.2 0.5 multiply_convert_fusion
  24.7 1.0 %fusion.17 = f32[32,128,128,1]{2,0,3,1:T(8,128)S(1)} fusion(bf16[4,6,128,128]{3,2,1,0:T(8,128)(2,1)S(1)} %multiply_convert_fusion, s32[4,6]{1,0:T(4,128)S(1)} %subtract_bitcast_fusion), kind=kOutput, calls=%fused_computation.24 | convolution fusion | flops 25166592 | bytes 2883680 | tf_op jit(solution)/shard_map/mctn,mcj->tjn/dot_general | solution.py:37
  25.9 3.2 %fusion.19 = (bf16[16,8,32,128]{3,1,2,0:T(8,128)(2,1)S(1)}, bf16[128,4096]{1,0:T(8,128)(2,1)}) fusion(f32[16,8,32,128]{3,2,1,0:T(8,128)S(1)} %bitcast.95, bf16[128,4096]{1,0:T(8,128)(2,1)S(1)} %copy-done), kind=kLoop, calls=%fused_computation.26 | loop fusion | flops 12058624 | bytes 5242880
  29.4 0.4 fusion.33
  30.6 5.0 %all_to_all.25 = f32[2,384,4,128]{3,1,2,0:T(8,128)S(1)} all-to-all(f32[2,384,4,128]{3,1,2,0:T(8,128)S(1)} %bitcast.96), channel_id=1, replica_groups=mesh['y'=8,'z'=12,'c'=2,'mp'=4] {'c'}, dimensions={0} | all-to-all | bytes 3145728 | tf_op jit(solution)/shard_map/all_to_all | solution.py:71
  35.6 0.9 reduce_sum.27
  36.5 1.8 %copy.117 = bf16[8,48,4,128]{3,1,2,0:T(8,128)(2,1)} copy(bf16[8,48,4,128]{3,1,0,2:T(8,128)(2,1)} %bitcast.103) | data formatting | bytes 786432 | tf_op jit(solution)/shard_map/convert_element_type | solution.py:73
  38.3 9.6 %all-to-all-start.2 = ((bf16[8,48,4,128]{3,1,2,0:T(8,128)(2,1)}), bf16[8,48,4,128]{3,1,2,0:T(8,128)(2,1)S(1)}, u32[]{:S(2)}, u32[]{:S(2)}) async-start(bf16[8,48,4,128]{3,1,2,0:T(8,128)(2,1)} %copy.117), calls=%async_computation.2 | async-start | bytes 786432 | tf_op jit(solution)/shard_map/all_to_all | solution.py:73
  48.0 0.7 fusion.29
  48.6 2.7 %fusion.13 = f32[4,8,128,128]{3,1,0,2:T(8,128)S(1)} fusion(f32[4,6,128,128]{3,2,1,0:T(8,128)S(1)} %fusion.29, s32[4,6]{1,0:T(4,128)S(1)} %get-tuple-element.12, pred[4,6]{1,0:T(4,128)(4,1)S(1)} %get-tuple-element.4), kind=kOutput, calls=%fused_computation.19 | convolution fusion | flops 150996480 | bytes 3670136 | tf_op jit(solution)/shard_map/mctk,mcr->rtk/dot_general | solution.py:52
  51.3 1.2 %dynamic-slice_bitcast_fusion.2 = (f32[8,128,128]{2,0,1:T(8,128)}, f32[8,128,128]{2,0,1:T(8,128)}, f32[8,128,128]{2,0,1:T(8,128)S(1)}) fusion(f32[4,8,128,128]{3,1,0,2:T(8,128)S(1)} %fusion.13, s32[]{:T(128)S(6)} %select_n.38, s32[]{:T(128)S(6)} %select_n.42, s32[]{:T(128)S(6)} %select_n.40), kind=kLoop, calls=%fused_computation.39 | loop fusion | bytes 3145740 | tf_op jit(solution)/shard_map/jit(dynamic_index_in_dim)/squeeze | solution.py:58
  52.5 2.5 %collective-permute-start = (f32[8,128,128]{2,0,1:T(8,128)}, f32[8,128,128]{2,0,1:T(8,128)S(1)}, u32[]{:S(2)}, u32[]{:S(2)}) collective-permute-start(f32[8,128,128]{2,0,1:T(8,128)} %get-tuple-element.5), channel_id=1, source_target_pairs={{0,1},{1,2},{2,3},{3,0},{4,5},{5,6},{6,7},{7,4},{8,9},{9,10},{10,1... | collective-permute-start | bytes 1572872 | tf_op jit(solution)/shard_map/ppermute | solution.py:60
  55.0 4.6 %collective-permute-start.2 = (f32[8,128,128]{2,0,1:T(8,128)}, f32[8,128,128]{2,0,1:T(8,128)}, u32[]{:S(2)}, u32[]{:S(2)}) collective-permute-start(f32[8,128,128]{2,0,1:T(8,128)} %get-tuple-element.6), channel_id=1, source_target_pairs={{0,3},{1,0},{2,1},{3,2},{4,7},{5,4},{6,5},{7,6},{8,11},{9,8},{10,9... | collective-permute-start | bytes 1572872 | tf_op jit(solution)/shard_map/ppermute | solution.py:60
  59.6 1.9 %collective-permute-start.1 = (f32[8,128,128]{2,0,1:T(8,128)S(1)}, f32[8,128,128]{2,0,1:T(8,128)}, u32[]{:S(2)}, u32[]{:S(2)}) collective-permute-start(f32[8,128,128]{2,0,1:T(8,128)S(1)} %get-tuple-element.7), channel_id=1, source_target_pairs={{0,2},{1,3},{2,0},{3,1},{4,6},{5,7},{6,4},{7,5},{8,10},{9,11},{10,... | collective-permute-start | bytes 1572872 | tf_op jit(solution)/shard_map/ppermute | solution.py:60
  61.8 0.7 copy.119
  62.5 12.8 %all-to-all-start.3 = ((f32[12,4,4,128]{3,1,2,0:T(4,128)}), f32[12,4,4,128]{3,1,2,0:T(4,128)S(1)}, u32[]{:S(2)}, u32[]{:S(2)}) async-start(f32[12,4,4,128]{3,1,2,0:T(4,128)} %copy.119), calls=%async_computation.3 | async-start | bytes 196608 | tf_op jit(solution)/shard_map/all_to_all | solution.py:75
  75.3 11.6 %all-to-all-done.3 = f32[12,4,4,128]{3,1,2,0:T(4,128)S(1)} async-done(((f32[12,4,4,128]{3,1,2,0:T(4,128)}), f32[12,4,4,128]{3,1,2,0:T(4,128)S(1)}, u32[]{:S(2)}, u32[]{:S(2)}) %all-to-all-start.3) | async-done | bytes 98336 | tf_op jit(solution)/shard_map/all_to_all | solution.py:75
  86.9 0.6 reduce_sum.29
  87.6 4.4 %all-to-all-start.4 = ((f32[4,4,128]{2,0,1:T(4,128)}), f32[4,4,128]{2,0,1:T(4,128)S(1)}, u32[]{:S(2)}, u32[]{:S(2)}) async-start(f32[4,4,128]{2,0,1:T(4,128)} %reduce_sum.29), calls=%async_computation.4 | async-start | bytes 16384 | tf_op jit(solution)/shard_map/all_to_all | solution.py:76
  92.0 1.3 %fusion.26 = bf16[8,128,128]{2,0,1:T(8,128)(2,1)S(1)} fusion(f32[8,128,128]{2,0,1:T(8,128)} %collective-permute-done.2, f32[8,128,128]{2,0,1:T(8,128)} %collective-permute-done.1, f32[8,128,128]{2,0,1:T(8,128)S(1)} %collective-permute-done, f32[4,8,128,128]{3,1,0,2:T(8,128)S(1)} %fusion.13, s32[]{:T(128)S(6)} %select_n.36), kind=kLoop, calls=%fused_computation.36 | loop fusion | flops 524288 | bytes 2359300 | tf_op jit(solution)/shard_map/convert_element_type | solution.py:61
  93.3 0.8 copy.154
  94.1 3.2 %all-to-all-done.4 = f32[4,4,128]{2,0,1:T(4,128)S(1)} async-done(((f32[4,4,128]{2,0,1:T(4,128)}), f32[4,4,128]{2,0,1:T(4,128)S(1)}, u32[]{:S(2)}, u32[]{:S(2)}) %all-to-all-start.4) | async-done | bytes 8224 | tf_op jit(solution)/shard_map/all_to_all | solution.py:76
  97.3 0.6 copy.156
  (27 shorter events, 2.6 us)
Async XLA Ops:
  0.6 7.3 %copy-start.1 = (bf16[128,4096]{1,0:T(8,128)(2,1)S(1)}, bf16[128,4096]{1,0:T(8,128)(2,1)}, u32[]{:S(2)}) copy-start(bf16[128,4096]{1,0:T(8,128)(2,1)} %param.5) | copy-start | bytes 3145732
  3.7 17.0 %all-to-all-start = ((bf16[4,784,128]{2,1,0:T(8,128)(2,1)}), bf16[4,784,128]{2,1,0:T(8,128)(2,1)}, u32[]{:S(2)}, u32[]{:S(2)}) async-start(bf16[4,784,128]{2,1,0:T(8,128)(2,1)} %fusion.20), calls=%async_computation | async-start | bytes 1605632 | tf_op jit(solution)/shard_map/all_to_all | solution.py:22
  24.7 1.2 %copy-start = (bf16[128,4096]{1,0:T(8,128)(2,1)S(1)}, bf16[128,4096]{1,0:T(8,128)(2,1)}, u32[]{:S(2)}) copy-start(bf16[128,4096]{1,0:T(8,128)(2,1)} %param.9) | copy-start | bytes 3145732
  38.3 23.5 %all-to-all-start.2 = ((bf16[8,48,4,128]{3,1,2,0:T(8,128)(2,1)}), bf16[8,48,4,128]{3,1,2,0:T(8,128)(2,1)S(1)}, u32[]{:S(2)}, u32[]{:S(2)}) async-start(bf16[8,48,4,128]{3,1,2,0:T(8,128)(2,1)} %copy.117), calls=%async_computation.2 | async-start | bytes 786432 | tf_op jit(solution)/shard_map/all_to_all | solution.py:73
  52.5 39.5 %collective-permute-start = (f32[8,128,128]{2,0,1:T(8,128)}, f32[8,128,128]{2,0,1:T(8,128)S(1)}, u32[]{:S(2)}, u32[]{:S(2)}) collective-permute-start(f32[8,128,128]{2,0,1:T(8,128)} %get-tuple-element.5), channel_id=1, source_target_pairs={{0,1},{1,2},{2,3},{3,0},{4,5},{5,6},{6,7},{7,4},{8,9},{9,10},{10,1... | collective-permute-start | bytes 1572872 | tf_op jit(solution)/shard_map/ppermute | solution.py:60
  55.0 37.0 %collective-permute-start.2 = (f32[8,128,128]{2,0,1:T(8,128)}, f32[8,128,128]{2,0,1:T(8,128)}, u32[]{:S(2)}, u32[]{:S(2)}) collective-permute-start(f32[8,128,128]{2,0,1:T(8,128)} %get-tuple-element.6), channel_id=1, source_target_pairs={{0,3},{1,0},{2,1},{3,2},{4,7},{5,4},{6,5},{7,6},{8,11},{9,8},{10,9... | collective-permute-start | bytes 1572872 | tf_op jit(solution)/shard_map/ppermute | solution.py:60
  59.6 32.4 %collective-permute-start.1 = (f32[8,128,128]{2,0,1:T(8,128)S(1)}, f32[8,128,128]{2,0,1:T(8,128)}, u32[]{:S(2)}, u32[]{:S(2)}) collective-permute-start(f32[8,128,128]{2,0,1:T(8,128)S(1)} %get-tuple-element.7), channel_id=1, source_target_pairs={{0,2},{1,3},{2,0},{3,1},{4,6},{5,7},{6,4},{7,5},{8,10},{9,11},{10,... | collective-permute-start | bytes 1572872 | tf_op jit(solution)/shard_map/ppermute | solution.py:60
  62.5 24.4 %all-to-all-start.3 = ((f32[12,4,4,128]{3,1,2,0:T(4,128)}), f32[12,4,4,128]{3,1,2,0:T(4,128)S(1)}, u32[]{:S(2)}, u32[]{:S(2)}) async-start(f32[12,4,4,128]{3,1,2,0:T(4,128)} %copy.119), calls=%async_computation.3 | async-start | bytes 196608 | tf_op jit(solution)/shard_map/all_to_all | solution.py:75
  87.6 9.7 %all-to-all-start.4 = ((f32[4,4,128]{2,0,1:T(4,128)}), f32[4,4,128]{2,0,1:T(4,128)S(1)}, u32[]{:S(2)}, u32[]{:S(2)}) async-start(f32[4,4,128]{2,0,1:T(4,128)} %reduce_sum.29), calls=%async_computation.4 | async-start | bytes 16384 | tf_op jit(solution)/shard_map/all_to_all | solution.py:76

commit v10 on v7

--- a/solution.py
+++ b/solution.py
@@ -68,7 +68,10 @@
     rows = slot_cap * block_size // (ny * nz * nc)
     staged = weight_terms.reshape(mp_count, ny, nz, nc, rows, block_size)
     staged = jnp.transpose(staged, (3, 1, 2, 4, 0, 5)).reshape(nc, -1, mp_count, block_size)
-    staged = lax.all_to_all(staged, "c", 0, 0, tiled=True).sum(0)
+    core_here = lax.axis_index("c")
+    mine = lax.dynamic_index_in_dim(staged, core_here, 0, keepdims=False)
+    other = lax.dynamic_index_in_dim(staged, 1 - core_here, 0, keepdims=False)
+    staged = mine + lax.ppermute(other, "c", [(0, 1), (1, 0)])
     staged = staged.reshape(ny * nz, rows, mp_count, block_size)
     staged = lax.all_to_all(staged.astype(jnp.bfloat16), ("y", "z"), 0, 0, tiled=True)
     staged = staged.astype(jnp.float32).sum(0)

time: 98.8 us -> 99 us (level)
  the two profiles are of different devices: /device:TPU:6 before, /device:TPU:7 now
where the time goes in v10:
time: 99 us; the launch traced here: 98.4 us
  starting transfers between devices  46.3 us (47%)
  waiting for transfers between devices  25.9 us (26%)
  local copies, waits for them, and re-layouts  10 us (10%)
  other arithmetic  9.49 us (10%)
  matrix products  5.77 us (6%)
    all_to_all x1, starting transfers between devices, body(): lax.all_to_all(staged.astype(jnp.bfloat16), ('y', 'z'), 0, 0, tiled=True)  15.9 us
    ppermute x1, starting transfers between devices, body(): staged = mine + lax.ppermute(other, 'c', [(0, 1), (1, 0)])  12.8 us
    ppermute x3, waiting for transfers between devices, body(): input_grad = input_grad + lax.ppermute(piece, 'mp', ring)  11.4 us
    ppermute x3, starting transfers between devices, body(): input_grad = input_grad + lax.ppermute(piece, 'mp', ring)  8.36 us
    all_to_all x1, waiting for transfers between devices, body(): lax.all_to_all(staged.astype(jnp.bfloat16), ('y', 'z'), 0, 0, tiled=True)  6.87 us
    all_to_all x1, waiting for transfers between devices, body(): lax.all_to_all(jnp.concatenate([w_groups, lists], 1), 'mp', 0, 0, tiled=T...  5.4 us
    all_to_all x1, starting transfers between devices, body(): staged = lax.all_to_all(staged, 'mp', 1, 1, tiled=True)  5.01 us
    all_to_all x1, starting transfers between devices, body(): lax.all_to_all(jnp.concatenate([w_groups, lists], 1), 'mp', 0, 0, tiled=T...  4.21 us
  transfers between devices with their start and end apart: 7, of which 4 were waited for; matrix products, arithmetic and copies ran while one was open for 9% of the time, Pallas kernels for 0%

profile of v10, /device:TPU:7, one launch (start us, length us, event | category | flops | bytes accessed | tf_op | source)
XLA Modules:
  0.0 98.4 jit_solution(10796352467852855114)
XLA Ops:
  0.6 0.8 convert_bitcast_fusion
  1.6 2.1 %fusion.20 = bf16[4,784,128]{2,1,0:T(8,128)(2,1)} fusion(bf16[4,1,12]{2,1,0:T(2,128)(2,1)S(1)} %convert_element_type.75, bf16[4,768,128]{2,1,0:T(8,128)(2,1)} %bitcast.111), kind=kLoop, calls=%fused_computation.27 | loop fusion | flops 2408448 | bytes 1589344 | tf_op jit(solution)/shard_map/concatenate | solution.py:22
  3.7 4.2 %all-to-all-start = ((bf16[4,784,128]{2,1,0:T(8,128)(2,1)}), bf16[4,784,128]{2,1,0:T(8,128)(2,1)}, u32[]{:S(2)}, u32[]{:S(2)}) async-start(bf16[4,784,128]{2,1,0:T(8,128)(2,1)} %fusion.20), calls=%async_computation | async-start | bytes 1605632 | tf_op jit(solution)/shard_map/all_to_all | solution.py:22
  7.9 0.7 copy.88
  8.6 0.7 copy.89
  9.2 5.4 %all-to-all-done = bf16[4,784,128]{2,1,0:T(8,128)(2,1)} async-done(((bf16[4,784,128]{2,1,0:T(8,128)(2,1)}), bf16[4,784,128]{2,1,0:T(8,128)(2,1)}, u32[]{:S(2)}, u32[]{:S(2)}) %all-to-all-start) | async-done | bytes 802848 | tf_op jit(solution)/shard_map/all_to_all | solution.py:22
  14.6 0.7 slice.18
  15.7 0.7 gather_fusion
  16.9 1.2 %slice.21 = bf16[4,768,128]{2,1,0:T(8,128)(2,1)S(1)} slice(bf16[4,784,128]{2,1,0:T(8,128)(2,1)} %all-to-all-done), slice={[0:4], [0:768], [0:128]} | slice | bytes 1572864 | tf_op jit(solution)/shard_map/slice | solution.py:23
  18.1 0.5 multiply_convert_fusion
  18.7 1.0 %fusion.17 = f32[32,128,128,1]{2,0,3,1:T(8,128)S(1)} fusion(bf16[4,6,128,128]{3,2,1,0:T(8,128)(2,1)S(1)} %multiply_convert_fusion, s32[4,6]{1,0:T(4,128)S(1)} %subtract_bitcast_fusion), kind=kOutput, calls=%fused_computation.24 | convolution fusion | flops 25166592 | bytes 2883680 | tf_op jit(solution)/shard_map/mctn,mcj->tjn/dot_general | solution.py:37
  19.9 3.2 %fusion.19 = (bf16[16,8,32,128]{3,1,2,0:T(8,128)(2,1)S(1)}, bf16[128,4096]{1,0:T(8,128)(2,1)}) fusion(f32[16,8,32,128]{3,2,1,0:T(8,128)S(1)} %bitcast.100, bf16[128,4096]{1,0:T(8,128)(2,1)S(1)} %copy-done), kind=kLoop, calls=%fused_computation.26 | loop fusion | flops 12058624 | bytes 5242880
  23.4 0.4 fusion.34
  24.6 1.0 dynamic-slice_bitcast_fusion
  25.5 12.8 %collective-permute-start.3 = (f32[384,4,128]{2,0,1:T(8,128)}, f32[384,4,128]{2,0,1:T(8,128)}, u32[]{:S(2)}, u32[]{:S(2)}) collective-permute-start(f32[384,4,128]{2,0,1:T(8,128)} %dynamic-slice_bitcast_fusion), channel_id=1, source_target_pairs={{0,4},{4,0},{1,5},{5,1},{2,6},{6,2},{3,7},{7,3},{8,12},{12,8},{9,1... | collective-permute-start | bytes 2359304 | tf_op jit(solution)/shard_map/ppermute | solution.py:74
  38.4 2.2 %collective-permute-done.3 = f32[384,4,128]{2,0,1:T(8,128)} collective-permute-done((f32[384,4,128]{2,0,1:T(8,128)}, f32[384,4,128]{2,0,1:T(8,128)}, u32[]{:S(2)}, u32[]{:S(2)}) %collective-permute-start.3) | collective-permute-done | bytes 786464 | tf_op jit(solution)/shard_map/ppermute | solution.py:74
  40.6 1.2 %fusion.21 = bf16[384,4,128]{2,0,1:T(8,128)(2,1)S(1)} fusion(f32[384,4,128]{2,0,1:T(8,128)} %collective-permute-done.3, f32[2,384,4,128]{3,1,2,0:T(8,128)S(1)} %bitcast.102, s32[]{:T(128)S(6)} %select_n.50), kind=kLoop, calls=%fused_computation.29 | loop fusion | flops 393216 | bytes 1966084 | tf_op jit(solution)/shard_map/convert_element_type | solution.py:76
  41.8 0.9 copy.96
  42.7 15.9 %all-to-all-start.1 = ((bf16[96,4,4,128]{3,1,2,0:T(4,128)(2,1)}), bf16[96,4,4,128]{3,1,2,0:T(4,128)(2,1)S(1)}, u32[]{:S(2)}, u32[]{:S(2)}) async-start(bf16[96,4,4,128]{3,1,2,0:T(4,128)(2,1)} %copy.96), calls=%async_computation.1 | async-start | bytes 786432 | tf_op jit(solution)/shard_map/all_to_all | solution.py:76
  58.6 0.7 fusion.30
  59.3 2.7 %fusion.13 = f32[4,8,128,128]{3,1,0,2:T(8,128)S(1)} fusion(f32[4,6,128,128]{3,2,1,0:T(8,128)S(1)} %fusion.30, s32[4,6]{1,0:T(4,128)S(1)} %get-tuple-element.12, pred[4,6]{1,0:T(4,128)(4,1)S(1)} %get-tuple-element.4), kind=kOutput, calls=%fused_computation.19 | convolution fusion | flops 150996480 | bytes 3670136 | tf_op jit(solution)/shard_map/mctk,mcr->rtk/dot_general | solution.py:52
  62.0 1.2 %dynamic-slice_bitcast_fusion.3 = (f32[8,128,128]{2,0,1:T(8,128)}, f32[8,128,128]{2,0,1:T(8,128)S(1)}, f32[8,128,128]{2,0,1:T(8,128)}) fusion(f32[4,8,128,128]{3,1,0,2:T(8,128)S(1)} %fusion.13, s32[]{:T(128)S(6)} %select_n.45, s32[]{:T(128)S(6)} %select_n.49, s32[]{:T(128)S(6)} %select_n.47), kind=kLoop, calls=%fused_computation.42 | loop fusion | bytes 3145740 | tf_op jit(solution)/shard_map/jit(dynamic_index_in_dim)/squeeze | solution.py:58
  63.2 3.7 %collective-permute-start = (f32[8,128,128]{2,0,1:T(8,128)}, f32[8,128,128]{2,0,1:T(8,128)S(1)}, u32[]{:S(2)}, u32[]{:S(2)}) collective-permute-start(f32[8,128,128]{2,0,1:T(8,128)} %get-tuple-element.5), channel_id=1, source_target_pairs={{0,1},{1,2},{2,3},{3,0},{4,5},{5,6},{6,7},{7,4},{8,9},{9,10},{10,1... | collective-permute-start | bytes 1572872 | tf_op jit(solution)/shard_map/ppermute | solution.py:60
  66.9 1.9 %collective-permute-start.1 = (f32[8,128,128]{2,0,1:T(8,128)}, f32[8,128,128]{2,0,1:T(8,128)}, u32[]{:S(2)}, u32[]{:S(2)}) collective-permute-start(f32[8,128,128]{2,0,1:T(8,128)} %get-tuple-element.7), channel_id=1, source_target_pairs={{0,2},{1,3},{2,0},{3,1},{4,6},{5,7},{6,4},{7,5},{8,10},{9,11},{10,... | collective-permute-start | bytes 1572872 | tf_op jit(solution)/shard_map/ppermute | solution.py:60
  68.8 2.8 %collective-permute-start.2 = (f32[8,128,128]{2,0,1:T(8,128)S(1)}, f32[8,128,128]{2,0,1:T(8,128)}, u32[]{:S(2)}, u32[]{:S(2)}) collective-permute-start(f32[8,128,128]{2,0,1:T(8,128)S(1)} %get-tuple-element.6), channel_id=1, source_target_pairs={{0,3},{1,0},{2,1},{3,2},{4,7},{5,4},{6,5},{7,6},{8,11},{9,8},{10,9... | collective-permute-start | bytes 1572872 | tf_op jit(solution)/shard_map/ppermute | solution.py:60
  71.6 6.9 %all-to-all-done.1 = bf16[96,4,4,128]{3,1,2,0:T(4,128)(2,1)S(1)} async-done(((bf16[96,4,4,128]{3,1,2,0:T(4,128)(2,1)}), bf16[96,4,4,128]{3,1,2,0:T(4,128)(2,1)S(1)}, u32[]{:S(2)}, u32[]{:S(2)}) %all-to-all-start.1) | async-done | bytes 393248 | tf_op jit(solution)/shard_map/all_to_all | solution.py:76
  78.4 0.8 convert_reduce_fusion
  79.2 5.0 %all-to-all-start.2 = ((f32[4,4,128]{2,0,1:T(4,128)}), f32[4,4,128]{2,0,1:T(4,128)S(1)}, u32[]{:S(2)}, u32[]{:S(2)}) async-start(f32[4,4,128]{2,0,1:T(4,128)} %convert_reduce_fusion), calls=%async_computation.2 | async-start | bytes 16384 | tf_op jit(solution)/shard_map/all_to_all | solution.py:78
  84.3 11.4 %collective-permute-done.2 = f32[8,128,128]{2,0,1:T(8,128)} collective-permute-done((f32[8,128,128]{2,0,1:T(8,128)S(1)}, f32[8,128,128]{2,0,1:T(8,128)}, u32[]{:S(2)}, u32[]{:S(2)}) %collective-permute-start.2) | collective-permute-done | bytes 524320 | tf_op jit(solution)/shard_map/ppermute | solution.py:60
  95.7 1.3 %fusion.27 = bf16[8,128,128]{2,0,1:T(8,128)(2,1)S(1)} fusion(f32[8,128,128]{2,0,1:T(8,128)} %collective-permute-done.2, f32[8,128,128]{2,0,1:T(8,128)} %collective-permute-done.1, f32[8,128,128]{2,0,1:T(8,128)S(1)} %collective-permute-done, f32[4,8,128,128]{3,1,0,2:T(8,128)S(1)} %fusion.13, s32[]{:T(128)S(6)} %select_n.43), kind=kLoop, calls=%fused_computation.39 | loop fusion | flops 524288 | bytes 2359300 | tf_op jit(solution)/shard_map/convert_element_type | solution.py:61
  97.0 0.8 copy.130
  97.8 0.6 copy.132
  (25 shorter events, 2.2 us)
Async XLA Ops:
  0.6 7.3 %copy-start.1 = (bf16[128,4096]{1,0:T(8,128)(2,1)S(1)}, bf16[128,4096]{1,0:T(8,128)(2,1)}, u32[]{:S(2)}) copy-start(bf16[128,4096]{1,0:T(8,128)(2,1)} %param.5) | copy-start | bytes 3145732
  3.7 11.0 %all-to-all-start = ((bf16[4,784,128]{2,1,0:T(8,128)(2,1)}), bf16[4,784,128]{2,1,0:T(8,128)(2,1)}, u32[]{:S(2)}, u32[]{:S(2)}) async-start(bf16[4,784,128]{2,1,0:T(8,128)(2,1)} %fusion.20), calls=%async_computation | async-start | bytes 1605632 | tf_op jit(solution)/shard_map/all_to_all | solution.py:22
  18.7 1.2 %copy-start = (bf16[128,4096]{1,0:T(8,128)(2,1)S(1)}, bf16[128,4096]{1,0:T(8,128)(2,1)}, u32[]{:S(2)}) copy-start(bf16[128,4096]{1,0:T(8,128)(2,1)} %param.9) | copy-start | bytes 3145732
  25.5 15.1 %collective-permute-start.3 = (f32[384,4,128]{2,0,1:T(8,128)}, f32[384,4,128]{2,0,1:T(8,128)}, u32[]{:S(2)}, u32[]{:S(2)}) collective-permute-start(f32[384,4,128]{2,0,1:T(8,128)} %dynamic-slice_bitcast_fusion), channel_id=1, source_target_pairs={{0,4},{4,0},{1,5},{5,1},{2,6},{6,2},{3,7},{7,3},{8,12},{12,8},{9,1... | collective-permute-start | bytes 2359304 | tf_op jit(solution)/shard_map/ppermute | solution.py:74
  42.7 35.7 %all-to-all-start.1 = ((bf16[96,4,4,128]{3,1,2,0:T(4,128)(2,1)}), bf16[96,4,4,128]{3,1,2,0:T(4,128)(2,1)S(1)}, u32[]{:S(2)}, u32[]{:S(2)}) async-start(bf16[96,4,4,128]{3,1,2,0:T(4,128)(2,1)} %copy.96), calls=%async_computation.1 | async-start | bytes 786432 | tf_op jit(solution)/shard_map/all_to_all | solution.py:76
  63.2 21.1 %collective-permute-start = (f32[8,128,128]{2,0,1:T(8,128)}, f32[8,128,128]{2,0,1:T(8,128)S(1)}, u32[]{:S(2)}, u32[]{:S(2)}) collective-permute-start(f32[8,128,128]{2,0,1:T(8,128)} %get-tuple-element.5), channel_id=1, source_target_pairs={{0,1},{1,2},{2,3},{3,0},{4,5},{5,6},{6,7},{7,4},{8,9},{9,10},{10,1... | collective-permute-start | bytes 1572872 | tf_op jit(solution)/shard_map/ppermute | solution.py:60
  66.9 17.4 %collective-permute-start.1 = (f32[8,128,128]{2,0,1:T(8,128)}, f32[8,128,128]{2,0,1:T(8,128)}, u32[]{:S(2)}, u32[]{:S(2)}) collective-permute-start(f32[8,128,128]{2,0,1:T(8,128)} %get-tuple-element.7), channel_id=1, source_target_pairs={{0,2},{1,3},{2,0},{3,1},{4,6},{5,7},{6,4},{7,5},{8,10},{9,11},{10,... | collective-permute-start | bytes 1572872 | tf_op jit(solution)/shard_map/ppermute | solution.py:60
  68.8 26.9 %collective-permute-start.2 = (f32[8,128,128]{2,0,1:T(8,128)S(1)}, f32[8,128,128]{2,0,1:T(8,128)}, u32[]{:S(2)}, u32[]{:S(2)}) collective-permute-start(f32[8,128,128]{2,0,1:T(8,128)S(1)} %get-tuple-element.6), channel_id=1, source_target_pairs={{0,3},{1,0},{2,1},{3,2},{4,7},{5,4},{6,5},{7,6},{8,11},{9,8},{10,9... | collective-permute-start | bytes 1572872 | tf_op jit(solution)/shard_map/ppermute | solution.py:60
  79.2 18.5 %all-to-all-start.2 = ((f32[4,4,128]{2,0,1:T(4,128)}), f32[4,4,128]{2,0,1:T(4,128)S(1)}, u32[]{:S(2)}, u32[]{:S(2)}) async-start(f32[4,4,128]{2,0,1:T(4,128)} %convert_reduce_fusion), calls=%async_computation.2 | async-start | bytes 16384 | tf_op jit(solution)/shard_map/all_to_all | solution.py:78

commit v11 on v7

--- a/solution.py
+++ b/solution.py
@@ -46,18 +46,18 @@
     input_terms = jnp.einsum(
         "mctn,mckn->mctk", grad_cols, w_here, preferred_element_type=jnp.float32
     )
+    local_row = (row_groups - column_here * (row_blocks // mp_count)) % row_blocks
     row_onehot = (
-        (row_groups[:, :, None] == jnp.arange(row_blocks)[None, None, :]) & slot_live[:, :, None]
+        (local_row[:, :, None] == jnp.arange(row_blocks)[None, None, :]) & slot_live[:, :, None]
     ).astype(jnp.float32)
     input_partial = jnp.einsum(
         "mctk,mcr->rtk", input_terms, row_onehot, precision=lax.Precision.HIGHEST
     )
     pieces = input_partial.reshape(mp_count, row_blocks // mp_count, token_count, block_size)
-    input_grad = lax.dynamic_index_in_dim(pieces, column_here, 0, keepdims=False)
+    input_grad = pieces[0]
     for shift in range(1, mp_count):
-        piece = lax.dynamic_index_in_dim(pieces, (column_here + shift) % mp_count, 0, keepdims=False)
         ring = [(k, (k + shift) % mp_count) for k in range(mp_count)]
-        input_grad = input_grad + lax.ppermute(piece, "mp", ring)
+        input_grad = input_grad + lax.ppermute(pieces[shift], "mp", ring)
     input_grad = jnp.transpose(input_grad.astype(jnp.bfloat16), (1, 0, 2))
     input_grad = input_grad.reshape(token_count, row_blocks * block_size // mp_count)
     weight_terms = jnp.einsum(

time: 98.8 us -> 98.7 us (level)
    squeeze x1 -> x0, local copies, waits for them, and re-layouts: 1.18 us -> none  [body(): lax.dynamic_index_in_dim(pieces, (column_here + shift) % mp_count, 0, kee...]
    slice x0 -> x1, local copies, waits for them, and re-layouts: none -> 1.07 us  [body(): input_grad = input_grad + lax.ppermute(pieces[shift], 'mp', ring)]
where the time goes in v11:
time: 98.7 us; the launch traced here: 98.1 us
  starting transfers between devices  44.9 us (45%)
  waiting for transfers between devices  22.4 us (23%)
  local copies, waits for them, and re-layouts  9.96 us (10%)
  other arithmetic  9.21 us (9%)
  matrix products  5.77 us (6%)
  blocking collectives  5 us (5%)
    all_to_all x1, starting transfers between devices, body(): lax.all_to_all(staged.astype(jnp.bfloat16), ('y', 'z'), 0, 0, tiled=True)  16.2 us
    all_to_all x1, starting transfers between devices, body(): lax.all_to_all(jnp.concatenate([w_groups, lists], 1), 'mp', 0, 0, tiled=T...  13.6 us
    ppermute x3, starting transfers between devices, body(): input_grad = input_grad + lax.ppermute(pieces[shift], 'mp', ring)  9.8 us
    all_to_all x1, waiting for transfers between devices, body(): lax.all_to_all(staged.astype(jnp.bfloat16), ('y', 'z'), 0, 0, tiled=True)  8.29 us
    ppermute x3, waiting for transfers between devices, body(): input_grad = input_grad + lax.ppermute(pieces[shift], 'mp', ring)  7.89 us
    all_to_all x1, waiting for transfers between devices, body(): lax.all_to_all(jnp.concatenate([w_groups, lists], 1), 'mp', 0, 0, tiled=T...  6.27 us
    all_to_all x1, starting transfers between devices, body(): staged = lax.all_to_all(staged, 'mp', 1, 1, tiled=True)  5.29 us
    all_to_all x1, blocking collectives, body(): staged = lax.all_to_all(staged, 'c', 0, 0, tiled=True).sum(0)  5 us
  transfers between devices with their start and end apart: 6, of which 4 were waited for; matrix products, arithmetic and copies ran while one was open for 9% of the time, Pallas kernels for 0%

profile of v11, /device:TPU:6, one launch (start us, length us, event | category | flops | bytes accessed | tf_op | source)
XLA Modules:
  0.0 98.1 jit_solution(3646468943374083947)
XLA Ops:
  0.6 0.8 convert_bitcast_fusion
  1.6 2.1 %fusion.20 = bf16[4,784,128]{2,1,0:T(8,128)(2,1)} fusion(bf16[4,1,12]{2,1,0:T(2,128)(2,1)S(1)} %convert_element_type.75, bf16[4,768,128]{2,1,0:T(8,128)(2,1)} %bitcast.88), kind=kLoop, calls=%fused_computation.27 | loop fusion | flops 2408448 | bytes 1589344 | tf_op jit(solution)/shard_map/concatenate | solution.py:22
  3.7 13.6 %all-to-all-start = ((bf16[4,784,128]{2,1,0:T(8,128)(2,1)}), bf16[4,784,128]{2,1,0:T(8,128)(2,1)}, u32[]{:S(2)}, u32[]{:S(2)}) async-start(bf16[4,784,128]{2,1,0:T(8,128)(2,1)} %fusion.20), calls=%async_computation | async-start | bytes 1605632 | tf_op jit(solution)/shard_map/all_to_all | solution.py:22
  17.3 0.7 copy.88
  18.0 0.7 copy.89
  18.6 6.3 %all-to-all-done = bf16[4,784,128]{2,1,0:T(8,128)(2,1)} async-done(((bf16[4,784,128]{2,1,0:T(8,128)(2,1)}), bf16[4,784,128]{2,1,0:T(8,128)(2,1)}, u32[]{:S(2)}, u32[]{:S(2)}) %all-to-all-start) | async-done | bytes 802848 | tf_op jit(solution)/shard_map/all_to_all | solution.py:22
  24.9 0.7 slice.38
  26.1 0.7 gather_fusion
  27.2 1.2 %slice.41 = bf16[4,768,128]{2,1,0:T(8,128)(2,1)S(1)} slice(bf16[4,784,128]{2,1,0:T(8,128)(2,1)} %all-to-all-done), slice={[0:4], [0:768], [0:128]} | slice | bytes 1572864 | tf_op jit(solution)/shard_map/slice | solution.py:23
  28.4 0.5 multiply_convert_fusion
  29.0 1.0 %fusion.17 = f32[32,128,128,1]{2,0,3,1:T(8,128)S(1)} fusion(bf16[4,6,128,128]{3,2,1,0:T(8,128)(2,1)S(1)} %multiply_convert_fusion, s32[4,6]{1,0:T(4,128)S(1)} %subtract_bitcast_fusion), kind=kOutput, calls=%fused_computation.24 | convolution fusion | flops 25166592 | bytes 2883680 | tf_op jit(solution)/shard_map/mctn,mcj->tjn/dot_general | solution.py:37
  30.2 3.2 %fusion.19 = (bf16[16,8,32,128]{3,1,2,0:T(8,128)(2,1)S(1)}, bf16[128,4096]{1,0:T(8,128)(2,1)}) fusion(f32[16,8,32,128]{3,2,1,0:T(8,128)S(1)} %bitcast.78, bf16[128,4096]{1,0:T(8,128)(2,1)S(1)} %copy-done), kind=kLoop, calls=%fused_computation.26 | loop fusion | flops 12058624 | bytes 5242880
  33.7 0.4 fusion.33
  34.1 0.4 fusion.21
  34.8 5.0 %all_to_all.20 = f32[2,384,4,128]{3,1,2,0:T(8,128)S(1)} all-to-all(f32[2,384,4,128]{3,1,2,0:T(8,128)S(1)} %bitcast.79), channel_id=1, replica_groups=mesh['y'=8,'z'=12,'c'=2,'mp'=4] {'c'}, dimensions={0} | all-to-all | bytes 3145728 | tf_op jit(solution)/shard_map/all_to_all | solution.py:71
  39.8 0.9 reduce_sum.18
  40.8 1.9 %copy.96 = bf16[96,4,4,128]{3,1,2,0:T(4,128)(2,1)} copy(bf16[96,4,4,128]{3,1,0,2:T(4,128)(2,1)} %bitcast.86) | data formatting | bytes 786432 | tf_op jit(solution)/shard_map/convert_element_type | solution.py:73
  42.7 16.2 %all-to-all-start.2 = ((bf16[96,4,4,128]{3,1,2,0:T(4,128)(2,1)}), bf16[96,4,4,128]{3,1,2,0:T(4,128)(2,1)S(1)}, u32[]{:S(2)}, u32[]{:S(2)}) async-start(bf16[96,4,4,128]{3,1,2,0:T(4,128)(2,1)} %copy.96), calls=%async_computation.2 | async-start | bytes 786432 | tf_op jit(solution)/shard_map/all_to_all | solution.py:73
  58.8 0.7 fusion.29
  59.5 2.7 %fusion.13 = f32[32,128,128]{2,0,1:T(8,128)S(1)} fusion(f32[4,6,128,128]{3,2,1,0:T(8,128)S(1)} %fusion.29, s32[4,6]{1,0:T(4,128)S(1)} %get-tuple-element.12, pred[4,6]{1,0:T(4,128)(4,1)S(1)} %get-tuple-element.4), kind=kOutput, calls=%fused_computation.19 | convolution fusion | flops 150996480 | bytes 3670136 | tf_op jit(solution)/shard_map/mctk,mcr->rtk/dot_general | solution.py:53
  62.2 1.1 %fusion.47 = (f32[8,128,128]{2,0,1:T(8,128)}, f32[8,128,128]{2,0,1:T(8,128)}, f32[8,128,128]{2,0,1:T(8,128)S(1)}) fusion(f32[32,128,128]{2,0,1:T(8,128)S(1)} %fusion.13), kind=kLoop, calls=%fused_computation.69 | loop fusion | bytes 3145728 | tf_op jit(solution)/shard_map/slice | solution.py:60
  63.3 4.0 %collective-permute-start = (f32[8,128,128]{2,0,1:T(8,128)}, f32[8,128,128]{2,0,1:T(8,128)S(1)}, u32[]{:S(2)}, u32[]{:S(2)}) collective-permute-start(f32[8,128,128]{2,0,1:T(8,128)} %get-tuple-element.5), channel_id=1, source_target_pairs={{0,1},{1,2},{2,3},{3,0},{4,5},{5,6},{6,7},{7,4},{8,9},{9,10},{10,1... | collective-permute-start | bytes 1572872 | tf_op jit(solution)/shard_map/ppermute | solution.py:60
  67.3 1.9 %collective-permute-start.2 = (f32[8,128,128]{2,0,1:T(8,128)}, f32[8,128,128]{2,0,1:T(8,128)}, u32[]{:S(2)}, u32[]{:S(2)}) collective-permute-start(f32[8,128,128]{2,0,1:T(8,128)} %get-tuple-element.6), channel_id=1, source_target_pairs={{0,3},{1,0},{2,1},{3,2},{4,7},{5,4},{6,5},{7,6},{8,11},{9,8},{10,9... | collective-permute-start | bytes 1572872 | tf_op jit(solution)/shard_map/ppermute | solution.py:60
  69.2 3.9 %collective-permute-start.1 = (f32[8,128,128]{2,0,1:T(8,128)S(1)}, f32[8,128,128]{2,0,1:T(8,128)}, u32[]{:S(2)}, u32[]{:S(2)}) collective-permute-start(f32[8,128,128]{2,0,1:T(8,128)S(1)} %get-tuple-element.7), channel_id=1, source_target_pairs={{0,2},{1,3},{2,0},{3,1},{4,6},{5,7},{6,4},{7,5},{8,10},{9,11},{10,... | collective-permute-start | bytes 1572872 | tf_op jit(solution)/shard_map/ppermute | solution.py:60
  73.1 8.3 %all-to-all-done.2 = bf16[96,4,4,128]{3,1,2,0:T(4,128)(2,1)S(1)} async-done(((bf16[96,4,4,128]{3,1,2,0:T(4,128)(2,1)}), bf16[96,4,4,128]{3,1,2,0:T(4,128)(2,1)S(1)}, u32[]{:S(2)}, u32[]{:S(2)}) %all-to-all-start.2) | async-done | bytes 393248 | tf_op jit(solution)/shard_map/all_to_all | solution.py:73
  81.4 0.8 convert_reduce_fusion
  82.2 5.3 %all-to-all-start.3 = ((f32[4,4,128]{2,0,1:T(4,128)}), f32[4,4,128]{2,0,1:T(4,128)S(1)}, u32[]{:S(2)}, u32[]{:S(2)}) async-start(f32[4,4,128]{2,0,1:T(4,128)} %convert_reduce_fusion), calls=%async_computation.3 | async-start | bytes 16384 | tf_op jit(solution)/shard_map/all_to_all | solution.py:75
  87.5 2.6 %collective-permute-done = f32[8,128,128]{2,0,1:T(8,128)S(1)} collective-permute-done((f32[8,128,128]{2,0,1:T(8,128)}, f32[8,128,128]{2,0,1:T(8,128)S(1)}, u32[]{:S(2)}, u32[]{:S(2)}) %collective-permute-start) | collective-permute-done | bytes 524320 | tf_op jit(solution)/shard_map/ppermute | solution.py:60
  90.1 5.3 %collective-permute-done.2 = f32[8,128,128]{2,0,1:T(8,128)} collective-permute-done((f32[8,128,128]{2,0,1:T(8,128)}, f32[8,128,128]{2,0,1:T(8,128)}, u32[]{:S(2)}, u32[]{:S(2)}) %collective-permute-start.2) | collective-permute-done | bytes 524320 | tf_op jit(solution)/shard_map/ppermute | solution.py:60
  95.4 1.3 %fusion.26 = bf16[8,128,128]{2,0,1:T(8,128)(2,1)S(1)} fusion(f32[8,128,128]{2,0,1:T(8,128)} %collective-permute-done.2, f32[8,128,128]{2,0,1:T(8,128)} %collective-permute-done.1, f32[8,128,128]{2,0,1:T(8,128)S(1)} %collective-permute-done, f32[32,128,128]{2,0,1:T(8,128)S(1)} %fusion.13), kind=kLoop, calls=%fused_computation.36 | loop fusion | flops 524288 | bytes 2359296 | tf_op jit(solution)/shard_map/convert_element_type | solution.py:61
  96.7 0.8 copy.130
  97.5 0.6 copy.132
  (23 shorter events, 1.8 us)
Async XLA Ops:
  0.6 16.7 %copy-start.1 = (bf16[128,4096]{1,0:T(8,128)(2,1)S(1)}, bf16[128,4096]{1,0:T(8,128)(2,1)}, u32[]{:S(2)}) copy-start(bf16[128,4096]{1,0:T(8,128)(2,1)} %param.5) | copy-start | bytes 3145732
  3.7 21.2 %all-to-all-start = ((bf16[4,784,128]{2,1,0:T(8,128)(2,1)}), bf16[4,784,128]{2,1,0:T(8,128)(2,1)}, u32[]{:S(2)}, u32[]{:S(2)}) async-start(bf16[4,784,128]{2,1,0:T(8,128)(2,1)} %fusion.20), calls=%async_computation | async-start | bytes 1605632 | tf_op jit(solution)/shard_map/all_to_all | solution.py:22
  28.9 1.2 %copy-start = (bf16[128,4096]{1,0:T(8,128)(2,1)S(1)}, bf16[128,4096]{1,0:T(8,128)(2,1)}, u32[]{:S(2)}) copy-start(bf16[128,4096]{1,0:T(8,128)(2,1)} %param.9) | copy-start | bytes 3145732
  42.7 38.7 %all-to-all-start.2 = ((bf16[96,4,4,128]{3,1,2,0:T(4,128)(2,1)}), bf16[96,4,4,128]{3,1,2,0:T(4,128)(2,1)S(1)}, u32[]{:S(2)}, u32[]{:S(2)}) async-start(bf16[96,4,4,128]{3,1,2,0:T(4,128)(2,1)} %copy.96), calls=%async_computation.2 | async-start | bytes 786432 | tf_op jit(solution)/shard_map/all_to_all | solution.py:73
  63.3 26.8 %collective-permute-start = (f32[8,128,128]{2,0,1:T(8,128)}, f32[8,128,128]{2,0,1:T(8,128)S(1)}, u32[]{:S(2)}, u32[]{:S(2)}) collective-permute-start(f32[8,128,128]{2,0,1:T(8,128)} %get-tuple-element.5), channel_id=1, source_target_pairs={{0,1},{1,2},{2,3},{3,0},{4,5},{5,6},{6,7},{7,4},{8,9},{9,10},{10,1... | collective-permute-start | bytes 1572872 | tf_op jit(solution)/shard_map/ppermute | solution.py:60
  67.3 28.1 %collective-permute-start.2 = (f32[8,128,128]{2,0,1:T(8,128)}, f32[8,128,128]{2,0,1:T(8,128)}, u32[]{:S(2)}, u32[]{:S(2)}) collective-permute-start(f32[8,128,128]{2,0,1:T(8,128)} %get-tuple-element.6), channel_id=1, source_target_pairs={{0,3},{1,0},{2,1},{3,2},{4,7},{5,4},{6,5},{7,6},{8,11},{9,8},{10,9... | collective-permute-start | bytes 1572872 | tf_op jit(solution)/shard_map/ppermute | solution.py:60
  69.2 26.2 %collective-permute-start.1 = (f32[8,128,128]{2,0,1:T(8,128)S(1)}, f32[8,128,128]{2,0,1:T(8,128)}, u32[]{:S(2)}, u32[]{:S(2)}) collective-permute-start(f32[8,128,128]{2,0,1:T(8,128)S(1)} %get-tuple-element.7), channel_id=1, source_target_pairs={{0,2},{1,3},{2,0},{3,1},{4,6},{5,7},{6,4},{7,5},{8,10},{9,11},{10,... | collective-permute-start | bytes 1572872 | tf_op jit(solution)/shard_map/ppermute | solution.py:60
  82.2 15.3 %all-to-all-start.3 = ((f32[4,4,128]{2,0,1:T(4,128)}), f32[4,4,128]{2,0,1:T(4,128)S(1)}, u32[]{:S(2)}, u32[]{:S(2)}) async-start(f32[4,4,128]{2,0,1:T(4,128)} %convert_reduce_fusion), calls=%async_computation.3 | async-start | bytes 16384 | tf_op jit(solution)/shard_map/all_to_all | solution.py:75
